TPU v7x, 1024 devices: a whole 4x8x16 slice. The times are simulated.
1024 devices in a mesh: pipe: 16 (over y, core), seq: 16 (over z), tp: 4 (over x).
Axes of the slice: x: 4, y: 8, z: 16, core: 2. Of those that a mesh axis runs over, the one named last changes fastest.
Arguments:
- emitted: bfloat16 [16, 2048, 8192], P('pipe', 'seq', 'tp'), may hold values from -6 to 6
- cotangent: bfloat16 [16, 2048, 8192], P('pipe', 'seq', 'tp'), may hold values from -6 to 6
- b_proj: bfloat16 [16, 2048, 512], P('pipe', 'seq', 'tp'), may hold values from -0.26367188 to 0.26367188
- c_proj: bfloat16 [16, 2048, 512], P('pipe', 'seq', 'tp'), may hold values from -0.52734375 to 0.52734375
- log_decay: bfloat16 [16, 2048, 128], P('pipe', 'seq', 'tp'), may hold values from -1 to 0
- starts: int32 [16, 2048], P('pipe', 'seq'), may hold values 0 or 1
- skip: float32 [16, 128], P('pipe', 'tp'), may hold values from 0.5 to 2
Outputs:
- mixed: bfloat16 [16, 2048, 8192], P('pipe', 'seq', 'tp')
- input_grad: bfloat16 [16, 2048, 8192], P('pipe', 'seq', 'tp')
All inputs are finite; a program needn't handle non-finite values. No bound on the sum of `starts` on one device may be relied on, other than what follows from the above.
Results may differ from a plain program's by a relative error of at most 0.001.
Values may be sent and summed in bfloat16 or wider, within the bound.
No kernel may reach another device: no remote copies, remote signals or barrier semaphores. Data moves between devices by JAX's collectives and lax.ppermute only.
A program may use at most 32 MiB of HBM per device.

v0:
```python
import jax
import jax.numpy as jnp
from jax import lax
from jax.sharding import PartitionSpec as P

BLEND_CHANNELS = 128
P_SIZE = 64
N = 128
GROUPS = 4
SPAN = 128


HIGH = lax.Precision.HIGHEST


def from_behind(value, axis, steps):
    count = lax.axis_size(axis)
    leading, last = (max(0, -steps), min(count, count - steps))
    return lax.ppermute(value, axis, [(source, source + steps) for source in range(leading, last)])


def single_terms(inputs, upstream, b_rows, c_rows, decay_rows, opened):
    running = jnp.cumsum(decay_rows, axis=1)
    running_end = running[:, -1]
    opened_sum = jnp.cumsum(opened, axis=1)
    opened_end = opened_sum[:, -1]
    width = inputs.shape[1]
    causal = jnp.arange(width)[:, None] >= jnp.arange(width)[None, :]
    linked = (opened_sum[:, :, None] == opened_sum[:, None, :]) & causal[None]
    spread = running[:, :, None] - running[:, None, :]
    damping = jnp.where(linked[:, :, :, None, None], jnp.exp(jnp.minimum(spread, 0.0)), 0.0)
    intersection = jnp.einsum("ktgn,ksgn->ktsg", c_rows, b_rows, precision=HIGH)
    mixing = damping * intersection[..., None]
    mixed_part = jnp.einsum("ktsge,ksgep->ktgep", mixing, inputs, precision=HIGH)
    grad_part = jnp.einsum("ktsge,ktgep->ksgep", mixing, upstream, precision=HIGH)
    inflow = jnp.exp(running) * (opened_sum == 0.0)[:, :, None, None]
    outflow = (
        jnp.exp(running_end[:, None] - running)
        * (opened_sum == opened_end[:, None])[:, :, None, None]
    )
    through = jnp.exp(running_end) * (opened_end == 0.0)[:, None, None]
    end_states = jnp.einsum(
        "ksgn,ksgep->kgenp", b_rows, inputs * outflow[..., None], precision=HIGH
    )
    start_states = jnp.einsum(
        "ksgn,ksgep->kgenp", c_rows, upstream * inflow[..., None], precision=HIGH
    )
    return (mixed_part, grad_part, inflow, outflow, through, end_states, start_states)


def block_terms(inputs, upstream, b_rows, c_rows, decay_rows, opened):

    def one_block(pieces):
        result = single_terms(*[piece[None] for piece in pieces])
        return tuple((item[0] for item in result))

    return lax.map(one_block, (inputs, upstream, b_rows, c_rows, decay_rows, opened))


def pass_forward(through, end_states, first_state):

    def advance(current, element):
        return (element[0][:, :, None, None] * current + element[1], current)

    final, entering = lax.scan(advance, first_state, (through, end_states))
    return (entering, final)


def pass_backward(through, start_states, last_state):

    def advance(current, element):
        return (element[0][:, :, None, None] * current + element[1], current)

    final, leaving = lax.scan(advance, last_state, (through, start_states), reverse=True)
    return (leaving, final)


def finish(terms, inputs, upstream, b_rows, c_rows, skip_gain, first_state, last_state):
    mixed_part, grad_part, inflow, outflow, through, end_states, start_states = terms
    entering, _ = pass_forward(through, end_states, first_state)
    leaving, _ = pass_backward(through, start_states, last_state)
    gain_wide = skip_gain[None, None, :, :, None]
    mixed = (
        mixed_part
        + jnp.einsum("ktgn,kgenp->ktgep", c_rows, entering, precision=HIGH) * inflow[..., None]
        + gain_wide * inputs
    )
    grads = (
        grad_part
        + jnp.einsum("ktgn,kgenp->ktgep", b_rows, leaving, precision=HIGH) * outflow[..., None]
        + gain_wide * upstream
    )
    return (mixed, grads)


def body(emitted, cotangent, b_proj, c_proj, log_decay, starts, skip):
    shifted = from_behind(emitted, "pipe", 1)
    inputs = jnp.where(lax.axis_index("pipe") == 0, emitted, shifted)[0]
    upstream = cotangent[0]
    length_dev = inputs.shape[0]
    local_heads = skip.shape[1]
    per_group = BLEND_CHANNELS // GROUPS
    seq_count = lax.axis_size("seq")
    head_share = local_heads // seq_count
    position = lax.axis_index("seq")
    flags = starts.astype(jnp.bfloat16)
    b_whole, c_whole, flag_whole = (
        lax.all_gather(b_proj, "seq", axis=1, tiled=True),
        lax.all_gather(c_proj, "seq", axis=1, tiled=True),
        lax.all_gather(flags, "seq", axis=1, tiled=True),
    )
    total_rows = length_dev * seq_count
    group_count = b_proj.shape[2] // N
    first_head = position * head_share
    group_pick = first_head // per_group
    b_rows = b_whole[0].reshape(total_rows, group_count, N)
    c_rows = c_whole[0].reshape(total_rows, group_count, N)
    outgoing = (
        inputs.reshape(length_dev, seq_count, head_share * P_SIZE),
        upstream.reshape(length_dev, seq_count, head_share * P_SIZE),
        log_decay[0].reshape(length_dev, seq_count, head_share),
    )
    got_inputs, got_upstream, got_decay = (
        lax.all_to_all(outgoing[0], "seq", split_axis=1, concat_axis=0, tiled=True),
        lax.all_to_all(outgoing[1], "seq", split_axis=1, concat_axis=0, tiled=True),
        lax.all_to_all(outgoing[2], "seq", split_axis=1, concat_axis=0, tiled=True),
    )
    block_count = total_rows // SPAN
    blocked = (block_count, SPAN, 1, head_share, P_SIZE)
    values = got_inputs.astype(jnp.float32).reshape(blocked)
    grads_in = got_upstream.astype(jnp.float32).reshape(blocked)
    b_blocks = b_rows.astype(jnp.float32).reshape(block_count, SPAN, 1, N)
    c_blocks = c_rows.astype(jnp.float32).reshape(block_count, SPAN, 1, N)
    decay_rows = got_decay.astype(jnp.float32).reshape(block_count, SPAN, 1, head_share)
    opened = flag_whole[0].astype(jnp.float32).reshape(block_count, SPAN)
    skip_gain = lax.dynamic_slice_in_dim(skip[0], first_head, head_share).reshape(1, head_share)
    terms = block_terms(values, grads_in, b_blocks, c_blocks, decay_rows, opened)
    empty_state = jnp.zeros((1, head_share, N, P_SIZE), jnp.float32)
    mixed, grads = finish(
        terms, values, grads_in, b_blocks, c_blocks, skip_gain, empty_state, empty_state
    )
    homeward = (
        mixed.reshape(total_rows, 1, head_share * P_SIZE).astype(jnp.bfloat16),
        grads.reshape(total_rows, 1, head_share * P_SIZE).astype(jnp.bfloat16),
    )
    mixed_back, grad_back = (
        lax.all_to_all(homeward[0], "seq", split_axis=0, concat_axis=1, tiled=True),
        lax.all_to_all(homeward[1], "seq", split_axis=0, concat_axis=1, tiled=True),
    )
    mixed_out = mixed_back.reshape(1, length_dev, local_heads * P_SIZE)
    grad_out = grad_back.reshape(1, length_dev, local_heads * P_SIZE)
    return (mixed_out, grad_out)


def solution(mesh):
    placed = (
        P("pipe", "seq", "tp"),
        P("pipe", "seq", "tp"),
        P("pipe", "seq", "tp"),
        P("pipe", "seq", "tp"),
        P("pipe", "seq", "tp"),
        P("pipe", "seq"),
        P("pipe", "tp"),
    )
    return jax.shard_map(
        body,
        mesh=mesh,
        in_specs=placed,
        out_specs=(P("pipe", "seq", "tp"), P("pipe", "seq", "tp")),
        check_vma=False,
    )
```

profile of v0, /device:TPU:60, one launch (start us, length us, event | category | flops | bytes accessed | tf_op | source)
XLA Modules:
  0.0 467.6 jit_solution(10548009101595904434)
XLA Ops:
  0.7 19.0 %all-to-all-start.1 = ((bf16[128,16,2]{0,2,1:T(2,128)(2,1)}), bf16[128,16,2]{0,2,1:T(2,128)(2,1)S(1)}, u32[]{:S(2)}, u32[]{:S(2)}) async-start(bf16[128,16,2]{0,2,1:T(2,128)(2,1)} %bitcast.265), calls=%async_computation.1 | async-start | bytes 16384 | tf_op jit(solution)/shard_map/all_to_all | solution.py:126
  19.7 2.0 copy.138
  21.7 10.3 %all-to-all-done.1 = bf16[128,16,2]{0,2,1:T(2,128)(2,1)S(1)} async-done(((bf16[128,16,2]{0,2,1:T(2,128)(2,1)}), bf16[128,16,2]{0,2,1:T(2,128)(2,1)S(1)}, u32[]{:S(2)}, u32[]{:S(2)}) %all-to-all-start.1) | async-done | bytes 8224 | tf_op jit(solution)/shard_map/all_to_all | solution.py:126
  32.1 3.6 all-to-all-start.2
  35.7 1.9 collective-permute-start
  37.6 8.6 %collective-permute-done = bf16[1,128,2048]{2,1,0:T(8,128)(2,1)S(1)} collective-permute-done((bf16[1,128,2048]{2,1,0:T(8,128)(2,1)S(1)}, bf16[1,128,2048]{2,1,0:T(8,128)(2,1)S(1)}, u32[]{:S(2)}, u32[]{:S(2)}) %collective-permute-start) | collective-permute-done | bytes 524320 | tf_op jit(solution)/shard_map/ppermute | solution.py:19
  47.2 15.1 %all-to-all-done.2 = bf16[128,16,128]{0,2,1:T(8,128)(2,1)S(1)} async-done(((bf16[128,16,128]{0,2,1:T(8,128)(2,1)}), bf16[128,16,128]{0,2,1:T(8,128)(2,1)S(1)}, u32[]{:S(2)}, u32[]{:S(2)}) %all-to-all-start.2) | async-done | bytes 524320 | tf_op jit(solution)/shard_map/all_to_all | solution.py:125
  62.4 7.5 %all-to-all-start = ((bf16[128,16,128]{0,2,1:T(8,128)(2,1)}), bf16[128,16,128]{0,2,1:T(8,128)(2,1)S(1)}, u32[]{:S(2)}, u32[]{:S(2)}) async-start(bf16[128,16,128]{0,2,1:T(8,128)(2,1)} %bitcast.25), calls=%async_computation | async-start | bytes 1048576 | tf_op jit(solution)/shard_map/all_to_all | solution.py:124
  69.9 51.1 %all_gather.10 = bf16[1,2048,128]{2,1,0:T(8,128)(2,1)S(1)} all-gather(bf16[1,128,128]{2,1,0:T(8,128)(2,1)S(1)} %copy-done.6), channel_id=1, replica_groups=mesh['pipe'=16,'seq'=16,'tp'=4] {'seq'}, dimensions={1}, use_global_device_ids=true | all-gather | bytes 557056 | tf_op jit(solution)/shard_map/all_gather | solution.py:108
  122.9 30.3 %all_gather.11 = bf16[1,2048,128]{2,1,0:T(8,128)(2,1)S(1)} all-gather(bf16[1,128,128]{2,1,0:T(8,128)(2,1)S(1)} %copy-done.7), channel_id=1, replica_groups=mesh['pipe'=16,'seq'=16,'tp'=4] {'seq'}, dimensions={1}, use_global_device_ids=true | all-gather | bytes 557056 | tf_op jit(solution)/shard_map/all_gather | solution.py:109
  154.3 27.9 %all_gather.9 = bf16[1,2048]{1,0:T(2,128)(2,1)S(1)} all-gather(bf16[1,128]{1,0:T(2,128)(2,1)S(1)} %convert_element_type.155), channel_id=1, replica_groups=mesh['pipe'=16,'seq'=16,'tp'=4] {'seq'}, dimensions={1}, use_global_device_ids=true | all-gather | bytes 4352 | tf_op jit(solution)/shard_map/all_gather | solution.py:110
  182.5 166.1 %while.52 = (s32[]{:T(128)}, f32[16,128,1,2,64]{1,4,3,2,0:T(8,128)}, f32[16,128,1,2,64]{1,4,3,2,0:T(8,128)}, f32[16,128,1,2]{3,2,1,0:T(1,128)}, f32[16,128,1,2]{...) while((s32[]{:T(128)}, ...), condition=%wide.region_3.4_spmd, body=%wide.region_0.3_spmd.sunk | while | flops 126224000 | bytes 1326827 | solution.py:57
  185.5 1.7 fusion.112
  216.7 1.7 fusion.112
  237.4 1.7 fusion.112
  247.8 1.7 fusion.112
  258.2 1.7 fusion.112
  279.0 1.7 fusion.112
  299.7 1.7 fusion.112
  310.1 1.7 fusion.112
  330.8 1.7 fusion.112
  350.2 17.5 %while.53 = (s32[]{:T(128)}, f32[1,2,128,64]{3,2,1,0:T(8,128)S(1)}, f32[16,1,2,128,64]{4,3,2,1,0:T(8,128)S(1)}, f32[16,1,2]{2,1,0:T(1,128)S(1)}, f32[16,1,2,128,64]{3,4,2,1,0:T(8,128)}, /*index=5*/s32[]{:T(128)}, s32[]{:T(128)}) while((s32[]{:T(128)}, f32[1,2,128,64]{3,2,1,0:T(8,128)S(1)}, f32[16,1,2,128,64]{4,3,2,1,0:T(8,128)S(1)}, ...), condition=%wide.region_5.6_spmd.clone, body=%wide.region_4.5_spmd.clone.sunk | while | flops 65539 | bytes 721020 | solution.py:65
  369.3 3.4 fusion.72
  374.7 11.5 %reduce = bf16[2048,128]{1,0:T(8,128)(2,1)S(1)} reduce(bf16[2048,1,128]{2,1,0:T(2,128)(2,1)S(1)} %reshape.513, bf16[]{:T(256)} %broadcast.236), dimensions={1}, to_apply=%reshape.513.reduce_sub_computation | reduce | bytes 1048578 | tf_op jit(solution)/shard_map/convert_element_type | solution.py:143
  387.2 8.9 %all-to-all-start.3 = ((bf16[16,2,8192]{2,1,0:T(2,128)(2,1)}), bf16[16,2,8192]{2,1,0:T(2,128)(2,1)}, u32[]{:S(2)}, u32[]{:S(2)}) async-start(bf16[16,2,8192]{2,1,0:T(2,128)(2,1)} %reshape.515), calls=%async_computation.3 | async-start | bytes 1048576 | tf_op jit(solution)/shard_map/all_to_all | solution.py:147
  396.4 17.7 %while.54 = (s32[]{:T(128)}, f32[1,2,128,64]{3,2,1,0:T(8,128)S(1)}, f32[16,1,2,128,64]{4,3,2,1,0:T(8,128)S(1)}, f32[16,1,2]{2,1,0:T(1,128)S(1)}, f32[16,1,2,128,...) while((s32[]{:T(128)}, f32[1,2,128,64]{3,2,1,0:T(8,128)S(1)}, ...), condition=%wide.region_7.8_spmd.clone, body=%wide.region_6.7_spmd.clone.sunk | while | flops 65540 | bytes 721040 | solution.py:74
  415.6 4.1 fusion.75
  419.7 2.4 copy.140
  422.7 11.5 %reduce.1 = bf16[2048,128]{1,0:T(8,128)(2,1)S(1)} reduce(bf16[2048,1,128]{2,1,0:T(2,128)(2,1)S(1)} %reshape.514, bf16[]{:T(256)} %broadcast.236), dimensions={1}, to_apply=%reshape.514.reduce_sub_computation | reduce | bytes 1048578 | tf_op jit(solution)/shard_map/convert_element_type | solution.py:144
  435.1 12.0 %all-to-all-start.4 = ((bf16[16,2,8192]{2,1,0:T(2,128)(2,1)}), bf16[16,2,8192]{2,1,0:T(2,128)(2,1)S(1)}, u32[]{:S(2)}, u32[]{:S(2)}) async-start(bf16[16,2,8192]{2,1,0:T(2,128)(2,1)} %reshape.517), calls=%async_computation.4 | async-start | bytes 1048576 | tf_op jit(solution)/shard_map/all_to_all | solution.py:148
  447.1 2.2 reshape.516
  450.7 15.0 %all-to-all-done.4 = bf16[16,2,8192]{2,1,0:T(2,128)(2,1)S(1)} async-done(((bf16[16,2,8192]{2,1,0:T(2,128)(2,1)}), bf16[16,2,8192]{2,1,0:T(2,128)(2,1)S(1)}, u32[]{:S(2)}, u32[]{:S(2)}) %all-to-all-start.4) | async-done | bytes 524320 | tf_op jit(solution)/shard_map/all_to_all | solution.py:148
  (511 shorter events, 190.2 us)
Async XLA Ops:
  0.6 181.6 %copy-start = (f32[1,32]{1,0:T(1,128)S(1)}, f32[1,32]{1,0:T(1,128)}, u32[]{:S(2)}) copy-start(f32[1,32]{1,0:T(1,128)} %param.19) | copy-start | bytes 388
  0.6 35.0 %copy-start.5 = (bf16[1,128,2048]{2,1,0:T(8,128)(2,1)S(1)}, bf16[1,128,2048]{2,1,0:T(8,128)(2,1)}, u32[]{:S(2)}) copy-start(bf16[1,128,2048]{2,1,0:T(8,128)(2,1)} %param.13) | copy-start | bytes 1572868
  0.7 31.4 %all-to-all-start.1 = ((bf16[128,16,2]{0,2,1:T(2,128)(2,1)}), bf16[128,16,2]{0,2,1:T(2,128)(2,1)S(1)}, u32[]{:S(2)}, u32[]{:S(2)}) async-start(bf16[128,16,2]{0,2,1:T(2,128)(2,1)} %bitcast.265), calls=%async_computation.1 | async-start | bytes 16384 | tf_op jit(solution)/shard_map/all_to_all | solution.py:126
  32.1 30.3 %all-to-all-start.2 = ((bf16[128,16,128]{0,2,1:T(8,128)(2,1)}), bf16[128,16,128]{0,2,1:T(8,128)(2,1)S(1)}, u32[]{:S(2)}, u32[]{:S(2)}) async-start(bf16[128,16,128]{0,2,1:T(8,128)(2,1)} %bitcast.36), calls=%async_computation.2 | async-start | bytes 1048576 | tf_op jit(solution)/shard_map/all_to_all | solution.py:125
  35.7 34.3 %copy-start.6 = (bf16[1,128,128]{2,1,0:T(8,128)(2,1)S(1)}, bf16[1,128,128]{2,1,0:T(8,128)(2,1)}, u32[]{:S(2)}) copy-start(bf16[1,128,128]{2,1,0:T(8,128)(2,1)} %param.15) | copy-start | bytes 98308
  35.7 10.5 %collective-permute-start = (bf16[1,128,2048]{2,1,0:T(8,128)(2,1)S(1)}, bf16[1,128,2048]{2,1,0:T(8,128)(2,1)S(1)}, u32[]{:S(2)}, u32[]{:S(2)}) collective-permute-start(bf16[1,128,2048]{2,1,0:T(8,128)(2,1)S(1)} %copy-done.5), channel_id=1, source_target_pairs={{0,64},{64,128},{128,192},{192,256},{256,320},{320,384},{384,448},... | collective-permute-start | bytes 1572872 | tf_op jit(solution)/shard_map/ppermute | solution.py:19
  46.2 76.7 %copy-start.7 = (bf16[1,128,128]{2,1,0:T(8,128)(2,1)S(1)}, bf16[1,128,128]{2,1,0:T(8,128)(2,1)}, u32[]{:S(2)}) copy-start(bf16[1,128,128]{2,1,0:T(8,128)(2,1)} %param.16) | copy-start | bytes 98308
  62.4 120.1 %all-to-all-start = ((bf16[128,16,128]{0,2,1:T(8,128)(2,1)}), bf16[128,16,128]{0,2,1:T(8,128)(2,1)S(1)}, u32[]{:S(2)}, u32[]{:S(2)}) async-start(bf16[128,16,128]{0,2,1:T(8,128)(2,1)} %bitcast.25), calls=%async_computation | async-start | bytes 1048576 | tf_op jit(solution)/shard_map/all_to_all | solution.py:124
  69.9 84.4 %copy-start.8 = (s32[1,128]{1,0:T(1,128)S(1)}, s32[1,128]{1,0:T(1,128)}, u32[]{:S(2)}) copy-start(s32[1,128]{1,0:T(1,128)} %param.18) | copy-start | bytes 1540
  121.0 0.8 copy-start.4
  348.6 1.0 copy-start.1
  348.6 1.3 copy-start.3
  387.2 47.9 %all-to-all-start.3 = ((bf16[16,2,8192]{2,1,0:T(2,128)(2,1)}), bf16[16,2,8192]{2,1,0:T(2,128)(2,1)}, u32[]{:S(2)}, u32[]{:S(2)}) async-start(bf16[16,2,8192]{2,1,0:T(2,128)(2,1)} %reshape.515), calls=%async_computation.3 | async-start | bytes 1048576 | tf_op jit(solution)/shard_map/all_to_all | solution.py:147
  396.4 19.2 %copy-start.2 = (f32[16,128,1,2,64]{1,4,3,2,0:T(8,128)S(1)}, f32[16,128,1,2,64]{1,4,3,2,0:T(8,128)}, u32[]{:S(2)}) copy-start(f32[16,128,1,2,64]{1,4,3,2,0:T(8,128)} %copy-done.1) | copy-start | bytes 3145732
  435.1 30.6 %all-to-all-start.4 = ((bf16[16,2,8192]{2,1,0:T(2,128)(2,1)}), bf16[16,2,8192]{2,1,0:T(2,128)(2,1)S(1)}, u32[]{:S(2)}, u32[]{:S(2)}) async-start(bf16[16,2,8192]{2,1,0:T(2,128)(2,1)} %reshape.517), calls=%async_computation.4 | async-start | bytes 1048576 | tf_op jit(solution)/shard_map/all_to_all | solution.py:148
where the time goes:
time: 473 us; the launch traced here: 468 us
  matrix products  112 us (24%)
  blocking collectives  109 us (23%)
  local copies, waits for them, and re-layouts  65.9 us (14%)
  other arithmetic  64.9 us (14%)
  starting transfers between devices  52.9 us (11%)
  waiting for transfers between devices  49 us (10%)
  loops' own time  12.9 us (3%)
    all_gather x1, blocking collectives, body(): lax.all_gather(b_proj, 'seq', axis=1, tiled=True)  51.1 us
    dynamic_slice x64, local copies, waits for them, and re-layouts, pass_forward(): final, entering = lax.scan(advance, first_state, (through, end_states))  30.4 us
    all_gather x1, blocking collectives, body(): lax.all_gather(c_proj, 'seq', axis=1, tiled=True)  30.3 us
    all_gather x1, blocking collectives, body(): lax.all_gather(flags, 'seq', axis=1, tiled=True)  27.9 us
    dot_general x16, matrix products, single_terms(): jnp.einsum('ksgn,ksgep->kgenp', b_rows, inputs * outflow[..., None], prec...  27.2 us
    dot_general x16, matrix products, single_terms(): jnp.einsum('ksgn,ksgep->kgenp', c_rows, upstream * inflow[..., None], pre...  26.7 us
    all_to_all x1, starting transfers between devices, body(): lax.all_to_all(outgoing[2], 'seq', split_axis=1, concat_axis=0, tiled=True)  19 us
    dot_general x16, matrix products, single_terms(): intersection = jnp.einsum('ktgn,ksgn->ktsg', c_rows, b_rows, precision=HIGH)  18.2 us
  transfers between devices with their start and end apart: 6, of which 4 were waited for; matrix products, arithmetic and copies ran while one was open for 10% of the time, Pallas kernels for 0%

commit v1 on v0

v1 whole, which is shorter than its diff:
```python
import jax
import jax.numpy as jnp
from jax import lax
from jax.sharding import PartitionSpec as P

BLEND_CHANNELS = 128
P_SIZE = 64
N = 128
GROUPS = 4
MISC = 16

F32 = jnp.float32
BF16 = jnp.bfloat16
HIGH = lax.Precision.HIGHEST


def from_behind(value, axis, steps):
    count = lax.axis_size(axis)
    leading, last = (max(0, -steps), min(count, count - steps))
    return lax.ppermute(value, axis, [(source, source + steps) for source in range(leading, last)])


def mm(spec, a, b):
    return jnp.einsum(spec, a, b, preferred_element_type=F32)


def mm_wide(spec, a, b):
    return jnp.einsum(spec, a.astype(F32), b.astype(F32), precision=HIGH)


mm_right = mm_wide
mm_left = mm_wide


def mix(xk, gk, bk, ck, deck, flk, gain):
    chunks, width = flk.shape
    order = jnp.arange(width)
    causal = order[:, None] >= order[None, :]
    tri = causal.astype(BF16)
    cum = mm("tu,khu->kht", tri, deck)
    seg = mm("tu,ku->kt", tri, flk)
    linked = (seg[:, :, None] == seg[:, None, :]) & causal[None]
    spread = cum[:, :, :, None] - cum[:, :, None, :]
    damping = jnp.where(linked[:, None], jnp.exp(jnp.minimum(spread, 0.0)), 0.0)
    overlap = mm("ktn,kun->ktu", ck, bk)
    mixing = damping * overlap[:, None]
    mixed = mm_left("khtu,kuhp->kthp", mixing, xk)
    grads = mm_left("khtu,kthp->kuhp", mixing, gk)

    cum_end = cum[:, :, -1]
    seg_end = seg[:, -1]
    outflow = jnp.exp(cum_end[:, :, None] - cum) * (seg == seg_end[:, None])[:, None, :]
    inflow = jnp.exp(cum) * (seg == 0.0)[:, None, :]
    outflow_q = outflow.transpose(0, 2, 1)[..., None]
    inflow_q = inflow.transpose(0, 2, 1)[..., None]
    end_states = mm_right("kun,kuhp->khnp", bk, outflow_q * xk.astype(F32))
    start_states = mm_right("ktn,kthp->khnp", ck, inflow_q * gk.astype(F32))

    total = jnp.cumsum(cum_end, axis=0)
    opened = jnp.cumsum((seg_end > 0.0).astype(F32))
    total_prev = jnp.concatenate([jnp.zeros_like(total[:1]), total[:-1]], axis=0)
    opened_prev = jnp.concatenate([jnp.zeros_like(opened[:1]), opened[:-1]], axis=0)
    index = jnp.arange(chunks)
    reach = (index[None, :] < index[:, None]) & (opened_prev[:, None] == opened[None, :])
    carry = jnp.where(
        reach[:, :, None],
        jnp.exp(jnp.minimum(total_prev[:, None, :] - total[None, :, :], 0.0)),
        0.0,
    )
    entering = jnp.einsum("kjh,jhnp->khnp", carry, end_states, precision=HIGH)
    leaving = jnp.einsum("jkh,jhnp->khnp", carry, start_states, precision=HIGH)

    mixed = mixed + inflow_q * mm_right("ktn,khnp->kthp", ck, entering)
    grads = grads + outflow_q * mm_right("kun,khnp->kuhp", bk, leaving)
    gain_wide = gain[None, None, :, None]
    mixed = mixed + gain_wide * xk.astype(F32)
    grads = grads + gain_wide * gk.astype(F32)
    return mixed, grads


def body(emitted, cotangent, b_proj, c_proj, log_decay, starts, skip):
    shifted = from_behind(emitted, "pipe", 1)
    inputs = jnp.where(lax.axis_index("pipe") == 0, emitted, shifted)[0]
    upstream = cotangent[0]
    length_dev = inputs.shape[0]
    seq_count = lax.axis_size("seq")
    local_heads = skip.shape[1]
    head_share = local_heads // seq_count
    lanes = head_share * P_SIZE
    per_group = BLEND_CHANNELS // GROUPS
    position = lax.axis_index("seq")
    first_head = position * head_share
    group_pick = first_head // per_group
    group_count = b_proj.shape[2] // N

    decay_rows = log_decay[0].reshape(length_dev, seq_count, head_share).transpose(1, 2, 0)
    flag_rows = jnp.broadcast_to(
        starts[0].astype(BF16)[None, None, :], (seq_count, 1, length_dev)
    )
    filler = jnp.zeros((seq_count, MISC - head_share - 1, length_dev), BF16)
    payload = jnp.concatenate(
        [
            inputs.reshape(length_dev, seq_count, lanes).transpose(1, 0, 2),
            upstream.reshape(length_dev, seq_count, lanes).transpose(1, 0, 2),
            decay_rows,
            flag_rows,
            filler,
        ],
        axis=1,
    )
    got = lax.all_to_all(payload, "seq", split_axis=0, concat_axis=0, tiled=True)

    proj = jnp.concatenate([b_proj[0], c_proj[0]], axis=-1)
    proj_whole = lax.all_gather(proj, "seq", axis=0, tiled=True)
    proj_whole = proj_whole.reshape(seq_count, length_dev, 2, group_count, N)
    proj_pick = lax.dynamic_index_in_dim(proj_whole, group_pick, axis=3, keepdims=False)
    bk = proj_pick[:, :, 0]
    ck = proj_pick[:, :, 1]

    xk = got[:, :length_dev].reshape(seq_count, length_dev, head_share, P_SIZE)
    gk = got[:, length_dev : 2 * length_dev].reshape(seq_count, length_dev, head_share, P_SIZE)
    deck = got[:, 2 * length_dev : 2 * length_dev + head_share]
    flk = got[:, 2 * length_dev + head_share]
    gain = lax.dynamic_slice_in_dim(skip[0], first_head, head_share)

    mixed, grads = mix(xk, gk, bk, ck, deck, flk, gain)
    homeward = jnp.concatenate(
        [
            mixed.reshape(seq_count, length_dev, lanes),
            grads.reshape(seq_count, length_dev, lanes),
        ],
        axis=1,
    ).astype(BF16)
    back = lax.all_to_all(homeward, "seq", split_axis=0, concat_axis=0, tiled=True)
    mixed_out = back[:, :length_dev].transpose(1, 0, 2).reshape(1, length_dev, local_heads * P_SIZE)
    grad_out = back[:, length_dev:].transpose(1, 0, 2).reshape(1, length_dev, local_heads * P_SIZE)
    return (mixed_out, grad_out)


def solution(mesh):
    placed = (
        P("pipe", "seq", "tp"),
        P("pipe", "seq", "tp"),
        P("pipe", "seq", "tp"),
        P("pipe", "seq", "tp"),
        P("pipe", "seq", "tp"),
        P("pipe", "seq"),
        P("pipe", "tp"),
    )
    return jax.shard_map(
        body,
        mesh=mesh,
        in_specs=placed,
        out_specs=(P("pipe", "seq", "tp"), P("pipe", "seq", "tp")),
        check_vma=False,
    )
```

time: 473 us -> 224 us (0.47)
  the two profiles are of different devices: /device:TPU:60 before, /device:TPU:92 now
where the time goes in v1:
time: 224 us; the launch traced here: 223 us
  waiting for transfers between devices  96.9 us (43%)
  blocking collectives  51.6 us (23%)
  local copies, waits for them, and re-layouts  22.5 us (10%)
  starting transfers between devices  20.5 us (9%)
  matrix products  15.5 us (7%)
  between operations  14.3 us (6%)
    all_gather x1, waiting for transfers between devices, body(): proj_whole = lax.all_gather(proj, 'seq', axis=0, tiled=True)  90 us
    all_to_all x1, blocking collectives, body(): lax.all_to_all(homeward, 'seq', split_axis=0, concat_axis=0, tiled=True)  51.6 us
    all_to_all x1, starting transfers between devices, body(): lax.all_to_all(payload, 'seq', split_axis=0, concat_axis=0, tiled=True)  18.6 us
    dot_general x4, matrix products, mm_wide(): return jnp.einsum(spec, a.astype(F32), b.astype(F32), precision=HIGH)  7.1 us
    ppermute x1, waiting for transfers between devices, from_behind(): lax.ppermute(value, axis, [(source, source + steps) for source in range(l...  6.9 us
    unnamed x21, local copies, waits for them, and re-layouts  5.4 us
  transfers between devices with their start and end apart: 3, of which 2 were waited for; matrix products, arithmetic and copies ran while one was open for 3% of the time, Pallas kernels for 0%

profile of v1, /device:TPU:92, one launch (start us, length us, event | category | flops | bytes accessed | tf_op | source)
XLA Modules:
  0.0 223.2 jit_solution(13920172235880905744)
XLA Ops:
  7.2 1.3 copy.54
  8.5 1.9 collective-permute-start
  10.5 1.3 copy.55
  12.1 6.9 %collective-permute-done = bf16[1,128,2048]{1,2,0:T(8,128)(2,1)S(1)} collective-permute-done((bf16[1,128,2048]{1,2,0:T(8,128)(2,1)S(1)}, bf16[1,128,2048]{1,2,0:T(8,128)(2,1)S(1)}, u32[]{:S(2)}, u32[]{:S(2)}) %collective-permute-start) | collective-permute-done | bytes 524320 | tf_op jit(solution)/shard_map/ppermute | solution.py:20
  19.1 1.0 broadcast_in_dim.16
  20.1 0.9 broadcast_in_dim.21
  21.0 2.7 %concatenate.16 = bf16[16,272,128]{1,2,0:T(8,128)(2,1)S(1)} concatenate(bf16[16,128,128]{1,2,0:T(8,128)(2,1)S(1)} %bitcast.111, bf16[16,128,128]{1,2,0:T(8,128)(2,1)S(1)} %bitcast.109, bf16[16,2,128]{1,2,0:T(8,128)(2,1)S(1)} %bitcast.110, bf16[16,1,128]{1,2,0:T(8,128)(2,1)} %broadcast_in_dim.16, bf16[16,13,128]{1,2,0:T(8,128)(2,1)} %broadcast_in_dim.21), dimensions={1} | concatenate | bytes 2228224 | tf_op jit(solution)/shard_map/concatenate | solution.py:101
  23.7 1.5 copy.57
  25.2 18.6 %all-to-all-start = ((bf16[16,272,128]{2,1,0:T(8,128)(2,1)}), bf16[16,272,128]{2,1,0:T(8,128)(2,1)}, u32[]{:S(2)}, u32[]{:S(2)}) async-start(bf16[16,272,128]{2,1,0:T(8,128)(2,1)} %copy.57), calls=%async_computation | async-start | bytes 2228224 | tf_op jit(solution)/shard_map/all_to_all | solution.py:111
  43.8 0.6 pad_maximum_fusion.1
  44.6 90.0 %all-gather.2.cloned.1.call-done = bf16[2048,256]{1,0:T(8,128)(2,1)} async-done(((bf16[128,256]{1,0:T(8,128)(2,1)}), bf16[2048,256]{1,0:T(8,128)(2,1)}) %all-gather.2.cloned.1.call-update) | async-done | bytes 1048592 | tf_op jit(solution)/shard_map/all_gather | solution.py:114
  134.6 1.3 reshape.125
  135.9 1.9 fusion.60
  137.9 1.5 fusion.26
  139.3 0.8 slice.53
  140.5 0.8 slice.54
  141.9 2.1 fusion.58
  144.0 1.3 copy.90
  145.9 0.7 convolution_bitcast_fusion.3
  146.7 1.7 convolution_bitcast_fusion.1
  148.4 0.3 copy.73
  148.8 2.2 fusion.28
  151.3 1.0 copy.95
  152.3 1.8 convolution_bitcast_fusion.2
  154.1 1.6 convolution_bitcast_fusion
  155.7 0.3 copy.76
  156.1 1.2 fusion.24
  157.6 2.7 %fusion.9 = bf16[16,128,2,64]{1,3,2,0:T(8,128)(2,1)S(1)} fusion(bf16[16,128,2,64]{1,3,2,0:T(8,128)(2,1)S(1)} %bitcast.104, f32[16,128,2,64]{1,3,2,0:T(8,128)S(1)} %bitcast.112, f32[16,128,128]{2,1,0:T(8,128)S(1)} %copy-done.2, f32[16,2,128]{2,1,0:T(2,128)S(1)} %copy.61, pred[16,128,128]{2,1,0:T(8,128)(4,1)S(1)} %compare_and_fusion, ...), kind=kOutput, calls=%fused_computation.18 | convolution fusion | flops 406323200 | bytes 3440648 | tf_op jit(solution)/shard_map/khtu,kuhp->kthp/dot_general | solution.py:28
  160.3 2.0 fusion.8
  162.4 51.6 %all_to_all.10 = bf16[16,256,128]{1,2,0:T(8,128)(2,1)S(1)} all-to-all(bf16[16,256,128]{1,2,0:T(8,128)(2,1)S(1)} %pad_maximum_fusion), channel_id=1, replica_groups=mesh['pipe'=16,'seq'=16,'tp'=4] {'seq'}, dimensions={0} | all-to-all | bytes 2097152 | tf_op jit(solution)/shard_map/all_to_all | solution.py:134
  214.3 1.0 copy.88
  215.3 1.0 copy.89
  (47 shorter events, 3.3 us)
Async XLA Ops:
  7.2 37.3 %copy-start = (f32[1,32]{1,0:T(1,128)S(1)}, f32[1,32]{1,0:T(1,128)}, u32[]{:S(2)}) copy-start(f32[1,32]{1,0:T(1,128)} %param.13) | copy-start | bytes 388
  7.2 4.6 %copy-start.6 = (bf16[1,128,32]{1,2,0:T(8,128)(2,1)S(1)}, bf16[1,128,32]{1,2,0:T(8,128)(2,1)}, u32[]{:S(2)}) copy-start(bf16[1,128,32]{1,2,0:T(8,128)(2,1)} %param.11) | copy-start | bytes 24580
  7.2 4.9 %copy-start.7 = (s32[1,128]{1,0:T(1,128)S(1)}, s32[1,128]{1,0:T(1,128)}, u32[]{:S(2)}) copy-start(s32[1,128]{1,0:T(1,128)} %param.12) | copy-start | bytes 1540
  8.5 10.5 %collective-permute-start = (bf16[1,128,2048]{1,2,0:T(8,128)(2,1)S(1)}, bf16[1,128,2048]{1,2,0:T(8,128)(2,1)S(1)}, u32[]{:S(2)}, u32[]{:S(2)}) collective-permute-start(bf16[1,128,2048]{1,2,0:T(8,128)(2,1)S(1)} %copy.54), channel_id=1, source_target_pairs={{0,64},{64,128},{128,192},{192,256},{256,320},{320,384},{384,448},... | collective-permute-start | bytes 1572872 | tf_op jit(solution)/shard_map/ppermute | solution.py:20
  25.2 18.6 %copy-start.4 = (bf16[1,128,128]{2,1,0:T(8,128)(2,1)S(1)}, bf16[1,128,128]{2,1,0:T(8,128)(2,1)}, u32[]{:S(2)}) copy-start(bf16[1,128,128]{2,1,0:T(8,128)(2,1)} %param.10) | copy-start | bytes 98308
  25.2 18.6 %copy-start.5 = (bf16[1,128,128]{2,1,0:T(8,128)(2,1)S(1)}, bf16[1,128,128]{2,1,0:T(8,128)(2,1)}, u32[]{:S(2)}) copy-start(bf16[1,128,128]{2,1,0:T(8,128)(2,1)} %param.9) | copy-start | bytes 98308
  25.2 114.2 %all-to-all-start = ((bf16[16,272,128]{2,1,0:T(8,128)(2,1)}), bf16[16,272,128]{2,1,0:T(8,128)(2,1)}, u32[]{:S(2)}, u32[]{:S(2)}) async-start(bf16[16,272,128]{2,1,0:T(8,128)(2,1)} %copy.57), calls=%async_computation | async-start | bytes 2228224 | tf_op jit(solution)/shard_map/all_to_all | solution.py:111
  43.8 90.8 %all-gather.2.cloned.1.call-start = ((), (), s32[]{:S(2)}) async-start(), calls=%async_computation.2 | async-start | bytes 1114112 | tf_op jit(solution)/shard_map/all_gather | solution.py:114
  156.1 1.2 copy-start.2
  156.1 1.5 copy-start.3
  157.6 2.7 %copy-start.1 = (bf16[16,128,128]{1,2,0:T(8,128)(2,1)S(1)}, bf16[16,128,128]{1,2,0:T(8,128)(2,1)}, u32[]{:S(2)}) copy-start(bf16[16,128,128]{1,2,0:T(8,128)(2,1)} %copy.95) | copy-start | bytes 1572868
Sparse Core Ops, SparseCore 0:
  47.8 86.7 all-gather.1

commit v2 on v1

--- a/solution.py
+++ b/solution.py
@@ -18,6 +18,26 @@
     count = lax.axis_size(axis)
     leading, last = (max(0, -steps), min(count, count - steps))
     return lax.ppermute(value, axis, [(source, source + steps) for source in range(leading, last)])
+
+
+def ring_shift(value, axis, steps):
+    count = lax.axis_size(axis)
+    return lax.ppermute(value, axis, [(source, (source + steps) % count) for source in range(count)])
+
+
+def ring_gather(block, axis, position):
+    count = lax.axis_size(axis)
+    ahead = count // 2
+    behind = count - 1 - ahead
+    from_left = [block]
+    from_right = [block]
+    for _ in range(ahead):
+        from_left.append(ring_shift(from_left[-1], axis, 1))
+    for _ in range(behind):
+        from_right.append(ring_shift(from_right[-1], axis, -1))
+    relative = [block] + from_right[1:] + from_left[1:][::-1]
+    stacked = jnp.stack(relative + relative, axis=0)
+    return lax.dynamic_slice_in_dim(stacked, (count - position) % count, count, axis=0)
 
 
 def mm(spec, a, b):
@@ -111,7 +131,7 @@
     got = lax.all_to_all(payload, "seq", split_axis=0, concat_axis=0, tiled=True)
 
     proj = jnp.concatenate([b_proj[0], c_proj[0]], axis=-1)
-    proj_whole = lax.all_gather(proj, "seq", axis=0, tiled=True)
+    proj_whole = ring_gather(proj, "seq", position)
     proj_whole = proj_whole.reshape(seq_count, length_dev, 2, group_count, N)
     proj_pick = lax.dynamic_index_in_dim(proj_whole, group_pick, axis=3, keepdims=False)
     bk = proj_pick[:, :, 0]

time: 224 us -> 226 us (level)
  the two profiles are of different devices: /device:TPU:92 before, /device:TPU:28 now
where the time goes in v2:
time: 226 us; the launch traced here: 225 us
  starting transfers between devices  72.2 us (32%)
  blocking collectives  59.9 us (27%)
  local copies, waits for them, and re-layouts  39.5 us (17%)
  waiting for transfers between devices  34.1 us (15%)
  matrix products  14.3 us (6%)
  other arithmetic  3.62 us (2%)
    ppermute x15, starting transfers between devices, ring_shift(): lax.ppermute(value, axis, [(source, (source + steps) % count) for source...  64.4 us
    all_to_all x1, blocking collectives, body(): lax.all_to_all(homeward, 'seq', split_axis=0, concat_axis=0, tiled=True)  59.9 us
    all_to_all x1, waiting for transfers between devices, body(): lax.all_to_all(payload, 'seq', split_axis=0, concat_axis=0, tiled=True)  28.9 us
    unnamed x78, local copies, waits for them, and re-layouts  27.2 us
    dot_general x4, matrix products, mm_wide(): return jnp.einsum(spec, a.astype(F32), b.astype(F32), precision=HIGH)  7.07 us
    all_to_all x1, starting transfers between devices, body(): lax.all_to_all(payload, 'seq', split_axis=0, concat_axis=0, tiled=True)  5.92 us
    ppermute x15, waiting for transfers between devices, ring_shift(): lax.ppermute(value, axis, [(source, (source + steps) % count) for source...  5.19 us
  transfers between devices with their start and end apart: 17, of which 3 were waited for; matrix products, arithmetic and copies ran while one was open for 16% of the time, Pallas kernels for 0%

profile of v2, /device:TPU:28, one launch (start us, length us, event | category | flops | bytes accessed | tf_op | source)
XLA Modules:
  0.0 224.9 jit_solution(15307826547349730098)
XLA Ops:
  2.4 18.2 %collective-permute-start.1 = (bf16[128,256]{0,1:T(8,128)(2,1)S(1)}, bf16[128,256]{0,1:T(8,128)(2,1)S(1)}, u32[]{:S(2)}, u32[]{:S(2)}) collective-permute-start(bf16[128,256]{0,1:T(8,128)(2,1)S(1)} %pad_maximum_fusion.1), channel_id=1, source_target_pairs={{0,60},{4,0},{8,4},{12,8},{16,12},{20,16},{24,20},{28,24},{32,28},... | collective-permute-start | bytes 196616 | tf_op jit(solution)/shard_map/ppermute | solution.py:25
  20.7 1.9 collective-permute-start.8
  23.9 1.9 collective-permute-start
  29.6 5.1 %collective-permute-start.2 = (bf16[128,256]{0,1:T(8,128)(2,1)S(1)}, bf16[128,256]{0,1:T(8,128)(2,1)S(1)}, u32[]{:S(2)}, u32[]{:S(2)}) collective-permute-start(bf16[128,256]{0,1:T(8,128)(2,1)S(1)} %collective-permute-done.1), channel_id=1, source_target_pairs={{0,60},{4,0},{8,4},{12,8},{16,12},{20,16},{24,20},{28,24},{32,28},... | collective-permute-start | bytes 196616 | tf_op jit(solution)/shard_map/ppermute | solution.py:25
  34.7 1.9 collective-permute-start.9
  37.2 5.1 %collective-permute-start.3 = (bf16[128,256]{0,1:T(8,128)(2,1)S(1)}, bf16[128,256]{0,1:T(8,128)(2,1)S(1)}, u32[]{:S(2)}, u32[]{:S(2)}) collective-permute-start(bf16[128,256]{0,1:T(8,128)(2,1)S(1)} %collective-permute-done.2), channel_id=1, source_target_pairs={{0,60},{4,0},{8,4},{12,8},{16,12},{20,16},{24,20},{28,24},{32,28},... | collective-permute-start | bytes 196616 | tf_op jit(solution)/shard_map/ppermute | solution.py:25
  42.4 1.9 collective-permute-start.10
  44.9 5.1 %collective-permute-start.4 = (bf16[128,256]{0,1:T(8,128)(2,1)S(1)}, bf16[128,256]{0,1:T(8,128)(2,1)S(1)}, u32[]{:S(2)}, u32[]{:S(2)}) collective-permute-start(bf16[128,256]{0,1:T(8,128)(2,1)S(1)} %collective-permute-done.3), channel_id=1, source_target_pairs={{0,60},{4,0},{8,4},{12,8},{16,12},{20,16},{24,20},{28,24},{32,28},... | collective-permute-start | bytes 196616 | tf_op jit(solution)/shard_map/ppermute | solution.py:25
  50.1 1.9 collective-permute-start.11
  52.6 5.1 %collective-permute-start.5 = (bf16[128,256]{0,1:T(8,128)(2,1)S(1)}, bf16[128,256]{0,1:T(8,128)(2,1)S(1)}, u32[]{:S(2)}, u32[]{:S(2)}) collective-permute-start(bf16[128,256]{0,1:T(8,128)(2,1)S(1)} %collective-permute-done.4), channel_id=1, source_target_pairs={{0,60},{4,0},{8,4},{12,8},{16,12},{20,16},{24,20},{28,24},{32,28},... | collective-permute-start | bytes 196616 | tf_op jit(solution)/shard_map/ppermute | solution.py:25
  57.8 1.9 collective-permute-start.12
  60.4 5.2 %collective-permute-start.6 = (bf16[128,256]{0,1:T(8,128)(2,1)S(1)}, bf16[128,256]{0,1:T(8,128)(2,1)S(1)}, u32[]{:S(2)}, u32[]{:S(2)}) collective-permute-start(bf16[128,256]{0,1:T(8,128)(2,1)S(1)} %collective-permute-done.5), channel_id=1, source_target_pairs={{0,60},{4,0},{8,4},{12,8},{16,12},{20,16},{24,20},{28,24},{32,28},... | collective-permute-start | bytes 196616 | tf_op jit(solution)/shard_map/ppermute | solution.py:25
  65.8 1.9 collective-permute-start.13
  68.4 5.1 %collective-permute-start.7 = (bf16[128,256]{0,1:T(8,128)(2,1)S(1)}, bf16[128,256]{0,1:T(8,128)(2,1)S(1)}, u32[]{:S(2)}, u32[]{:S(2)}) collective-permute-start(bf16[128,256]{0,1:T(8,128)(2,1)S(1)} %collective-permute-done.6), channel_id=1, source_target_pairs={{0,60},{4,0},{8,4},{12,8},{16,12},{20,16},{24,20},{28,24},{32,28},... | collective-permute-start | bytes 196616 | tf_op jit(solution)/shard_map/ppermute | solution.py:25
  73.5 1.9 collective-permute-start.14
  76.1 4.9 %collective-permute-done.14 = bf16[128,256]{0,1:T(8,128)(2,1)} collective-permute-done((bf16[128,256]{0,1:T(8,128)(2,1)S(1)}, bf16[128,256]{0,1:T(8,128)(2,1)}, u32[]{:S(2)}, u32[]{:S(2)}) %collective-permute-start.14) | collective-permute-done | bytes 65568 | tf_op jit(solution)/shard_map/ppermute | solution.py:25
  81.0 1.9 collective-permute-start.15
  85.5 2.7 %concatenate.16 = bf16[16,272,128]{1,2,0:T(8,128)(2,1)S(1)} concatenate(bf16[16,128,128]{1,2,0:T(8,128)(2,1)S(1)} %bitcast.171, bf16[16,128,128]{1,2,0:T(8,128)(2,1)S(1)} %bitcast.169, bf16[16,2,128]{1,2,0:T(8,128)(2,1)S(1)} %bitcast.170, bf16[16,1,128]{1,2,0:T(8,128)(2,1)} %broadcast_in_dim.16, bf16[16,13,128]{1,2,0:T(8,128)(2,1)} %broadcast_in_dim.21), dimensions={1} | concatenate | bytes 2228224 | tf_op jit(solution)/shard_map/concatenate | solution.py:121
  88.2 1.6 copy.59
  89.8 5.9 %all-to-all-start = ((bf16[16,272,128]{2,1,0:T(8,128)(2,1)}), bf16[16,272,128]{2,1,0:T(8,128)(2,1)S(1)}, u32[]{:S(2)}, u32[]{:S(2)}) async-start(bf16[16,272,128]{2,1,0:T(8,128)(2,1)} %copy.59), calls=%async_computation | async-start | bytes 2228224 | tf_op jit(solution)/shard_map/all_to_all | solution.py:131
  95.8 1.5 constant_dynamic-update-slice_fusion.23
  97.2 1.5 constant_dynamic-update-slice_fusion.22
  107.5 1.5 constant_dynamic-update-slice_fusion.7
  108.9 1.5 constant_dynamic-update-slice_fusion.6
  115.4 1.4 fusion.26
  116.8 28.9 %all-to-all-done = bf16[16,272,128]{2,1,0:T(8,128)(2,1)S(1)} async-done(((bf16[16,272,128]{2,1,0:T(8,128)(2,1)}), bf16[16,272,128]{2,1,0:T(8,128)(2,1)S(1)}, u32[]{:S(2)}, u32[]{:S(2)}) %all-to-all-start) | async-done | bytes 1114144 | tf_op jit(solution)/shard_map/all_to_all | solution.py:131
  149.2 1.7 convolution_bitcast_fusion.1
  151.2 1.6 fusion.28
  154.7 1.6 convolution_bitcast_fusion
  157.9 2.7 %fusion.9 = bf16[16,128,2,64]{1,3,2,0:T(8,128)(2,1)S(1)} fusion(bf16[16,128,2,64]{1,3,2,0:T(8,128)(2,1)S(1)} %bitcast.164, f32[16,128,2,64]{1,3,2,0:T(8,128)S(1)} %bitcast.172, f32[16,128,128]{2,1,0:T(8,128)S(1)} %copy-done.1, f32[16,2,128]{2,1,0:T(2,128)S(1)} %copy.63, pred[16,128,128]{2,1,0:T(8,128)(4,1)S(1)} %compare_and_fusion, ...), kind=kOutput, calls=%fused_computation.18 | convolution fusion | flops 406323200 | bytes 3440648 | tf_op jit(solution)/shard_map/khtu,kuhp->kthp/dot_general | solution.py:48
  160.6 1.9 fusion.8
  162.7 59.9 %all_to_all.10 = bf16[16,256,128]{1,2,0:T(8,128)(2,1)S(1)} all-to-all(bf16[16,256,128]{1,2,0:T(8,128)(2,1)S(1)} %pad_maximum_fusion), channel_id=1, replica_groups=mesh['pipe'=16,'seq'=16,'tp'=4] {'seq'}, dimensions={0} | all-to-all | bytes 2097152 | tf_op jit(solution)/shard_map/all_to_all | solution.py:154
  (133 shorter events, 36.7 us)
Async XLA Ops:
  0.6 28.8 %copy-start = (f32[1,32]{1,0:T(1,128)S(1)}, f32[1,32]{1,0:T(1,128)}, u32[]{:S(2)}) copy-start(f32[1,32]{1,0:T(1,128)} %param.13) | copy-start | bytes 388
  0.6 28.4 %copy-start.20 = (bf16[1,128,32]{1,2,0:T(8,128)(2,1)S(1)}, bf16[1,128,32]{1,2,0:T(8,128)(2,1)}, u32[]{:S(2)}) copy-start(bf16[1,128,32]{1,2,0:T(8,128)(2,1)} %param.11) | copy-start | bytes 24580
  2.4 27.1 %collective-permute-start.1 = (bf16[128,256]{0,1:T(8,128)(2,1)S(1)}, bf16[128,256]{0,1:T(8,128)(2,1)S(1)}, u32[]{:S(2)}, u32[]{:S(2)}) collective-permute-start(bf16[128,256]{0,1:T(8,128)(2,1)S(1)} %pad_maximum_fusion.1), channel_id=1, source_target_pairs={{0,60},{4,0},{8,4},{12,8},{16,12},{20,16},{24,20},{28,24},{32,28},... | collective-permute-start | bytes 196616 | tf_op jit(solution)/shard_map/ppermute | solution.py:25
  20.7 14.0 %collective-permute-start.8 = (bf16[128,256]{0,1:T(8,128)(2,1)S(1)}, bf16[128,256]{0,1:T(8,128)(2,1)S(1)}, u32[]{:S(2)}, u32[]{:S(2)}) collective-permute-start(bf16[128,256]{0,1:T(8,128)(2,1)S(1)} %pad_maximum_fusion.1), channel_id=1, source_target_pairs={{0,4},{4,8},{8,12},{12,16},{16,20},{20,24},{24,28},{28,32},{32,36}... | collective-permute-start | bytes 196616 | tf_op jit(solution)/shard_map/ppermute | solution.py:25
  23.9 59.6 %collective-permute-start = (bf16[1,128,2048]{1,2,0:T(8,128)(2,1)S(1)}, bf16[1,128,2048]{1,2,0:T(8,128)(2,1)S(1)}, u32[]{:S(2)}, u32[]{:S(2)}) collective-permute-start(bf16[1,128,2048]{1,2,0:T(8,128)(2,1)S(1)} %copy.56), channel_id=1, source_target_pairs={{0,64},{64,128},{128,192},{192,256},{256,320},{320,384},{384,448},... | collective-permute-start | bytes 1572872 | tf_op jit(solution)/shard_map/ppermute | solution.py:20
  29.6 7.7 %collective-permute-start.2 = (bf16[128,256]{0,1:T(8,128)(2,1)S(1)}, bf16[128,256]{0,1:T(8,128)(2,1)S(1)}, u32[]{:S(2)}, u32[]{:S(2)}) collective-permute-start(bf16[128,256]{0,1:T(8,128)(2,1)S(1)} %collective-permute-done.1), channel_id=1, source_target_pairs={{0,60},{4,0},{8,4},{12,8},{16,12},{20,16},{24,20},{28,24},{32,28},... | collective-permute-start | bytes 196616 | tf_op jit(solution)/shard_map/ppermute | solution.py:25
  34.7 7.7 %collective-permute-start.9 = (bf16[128,256]{0,1:T(8,128)(2,1)S(1)}, bf16[128,256]{0,1:T(8,128)(2,1)S(1)}, u32[]{:S(2)}, u32[]{:S(2)}) collective-permute-start(bf16[128,256]{0,1:T(8,128)(2,1)S(1)} %collective-permute-done.8), channel_id=1, source_target_pairs={{0,4},{4,8},{8,12},{12,16},{16,20},{20,24},{24,28},{28,32},{32,36}... | collective-permute-start | bytes 196616 | tf_op jit(solution)/shard_map/ppermute | solution.py:25
  37.2 7.7 %collective-permute-start.3 = (bf16[128,256]{0,1:T(8,128)(2,1)S(1)}, bf16[128,256]{0,1:T(8,128)(2,1)S(1)}, u32[]{:S(2)}, u32[]{:S(2)}) collective-permute-start(bf16[128,256]{0,1:T(8,128)(2,1)S(1)} %collective-permute-done.2), channel_id=1, source_target_pairs={{0,60},{4,0},{8,4},{12,8},{16,12},{20,16},{24,20},{28,24},{32,28},... | collective-permute-start | bytes 196616 | tf_op jit(solution)/shard_map/ppermute | solution.py:25
  42.4 7.7 %collective-permute-start.10 = (bf16[128,256]{0,1:T(8,128)(2,1)S(1)}, bf16[128,256]{0,1:T(8,128)(2,1)S(1)}, u32[]{:S(2)}, u32[]{:S(2)}) collective-permute-start(bf16[128,256]{0,1:T(8,128)(2,1)S(1)} %collective-permute-done.9), channel_id=1, source_target_pairs={{0,4},{4,8},{8,12},{12,16},{16,20},{20,24},{24,28},{28,32},{32,36}... | collective-permute-start | bytes 196616 | tf_op jit(solution)/shard_map/ppermute | solution.py:25
  44.9 39.7 %copy-start.5 = (bf16[128,256]{0,1:T(8,128)(2,1)}, bf16[128,256]{0,1:T(8,128)(2,1)S(1)}, u32[]{:S(2)}) copy-start(bf16[128,256]{0,1:T(8,128)(2,1)S(1)} %collective-permute-done.3) | copy-start | bytes 196612
  44.9 7.7 %collective-permute-start.4 = (bf16[128,256]{0,1:T(8,128)(2,1)S(1)}, bf16[128,256]{0,1:T(8,128)(2,1)S(1)}, u32[]{:S(2)}, u32[]{:S(2)}) collective-permute-start(bf16[128,256]{0,1:T(8,128)(2,1)S(1)} %collective-permute-done.3), channel_id=1, source_target_pairs={{0,60},{4,0},{8,4},{12,8},{16,12},{20,16},{24,20},{28,24},{32,28},... | collective-permute-start | bytes 196616 | tf_op jit(solution)/shard_map/ppermute | solution.py:25
  50.1 7.7 %collective-permute-start.11 = (bf16[128,256]{0,1:T(8,128)(2,1)S(1)}, bf16[128,256]{0,1:T(8,128)(2,1)S(1)}, u32[]{:S(2)}, u32[]{:S(2)}) collective-permute-start(bf16[128,256]{0,1:T(8,128)(2,1)S(1)} %collective-permute-done.10), channel_id=1, source_target_pairs={{0,4},{4,8},{8,12},{12,16},{16,20},{20,24},{24,28},{28,32},{32,36}... | collective-permute-start | bytes 196616 | tf_op jit(solution)/shard_map/ppermute | solution.py:25
  52.6 32.0 %copy-start.7 = (bf16[128,256]{0,1:T(8,128)(2,1)}, bf16[128,256]{0,1:T(8,128)(2,1)S(1)}, u32[]{:S(2)}) copy-start(bf16[128,256]{0,1:T(8,128)(2,1)S(1)} %collective-permute-done.4) | copy-start | bytes 196612
  52.6 7.7 %collective-permute-start.5 = (bf16[128,256]{0,1:T(8,128)(2,1)S(1)}, bf16[128,256]{0,1:T(8,128)(2,1)S(1)}, u32[]{:S(2)}, u32[]{:S(2)}) collective-permute-start(bf16[128,256]{0,1:T(8,128)(2,1)S(1)} %collective-permute-done.4), channel_id=1, source_target_pairs={{0,60},{4,0},{8,4},{12,8},{16,12},{20,16},{24,20},{28,24},{32,28},... | collective-permute-start | bytes 196616 | tf_op jit(solution)/shard_map/ppermute | solution.py:25
  57.8 26.8 %copy-start.3 = (bf16[128,256]{0,1:T(8,128)(2,1)}, bf16[128,256]{0,1:T(8,128)(2,1)S(1)}, u32[]{:S(2)}) copy-start(bf16[128,256]{0,1:T(8,128)(2,1)S(1)} %collective-permute-done.11) | copy-start | bytes 196612
  57.8 8.0 %collective-permute-start.12 = (bf16[128,256]{0,1:T(8,128)(2,1)S(1)}, bf16[128,256]{0,1:T(8,128)(2,1)S(1)}, u32[]{:S(2)}, u32[]{:S(2)}) collective-permute-start(bf16[128,256]{0,1:T(8,128)(2,1)S(1)} %collective-permute-done.11), channel_id=1, source_target_pairs={{0,4},{4,8},{8,12},{12,16},{16,20},{20,24},{24,28},{28,32},{32,36}... | collective-permute-start | bytes 196616 | tf_op jit(solution)/shard_map/ppermute | solution.py:25
  60.4 24.2 %copy-start.11 = (bf16[128,256]{0,1:T(8,128)(2,1)}, bf16[128,256]{0,1:T(8,128)(2,1)S(1)}, u32[]{:S(2)}) copy-start(bf16[128,256]{0,1:T(8,128)(2,1)S(1)} %collective-permute-done.5) | copy-start | bytes 196612
  60.4 8.0 %collective-permute-start.6 = (bf16[128,256]{0,1:T(8,128)(2,1)S(1)}, bf16[128,256]{0,1:T(8,128)(2,1)S(1)}, u32[]{:S(2)}, u32[]{:S(2)}) collective-permute-start(bf16[128,256]{0,1:T(8,128)(2,1)S(1)} %collective-permute-done.5), channel_id=1, source_target_pairs={{0,60},{4,0},{8,4},{12,8},{16,12},{20,16},{24,20},{28,24},{32,28},... | collective-permute-start | bytes 196616 | tf_op jit(solution)/shard_map/ppermute | solution.py:25
  65.8 18.8 %copy-start.9 = (bf16[128,256]{0,1:T(8,128)(2,1)}, bf16[128,256]{0,1:T(8,128)(2,1)S(1)}, u32[]{:S(2)}) copy-start(bf16[128,256]{0,1:T(8,128)(2,1)S(1)} %collective-permute-done.12) | copy-start | bytes 196612
  65.8 7.7 %collective-permute-start.13 = (bf16[128,256]{0,1:T(8,128)(2,1)S(1)}, bf16[128,256]{0,1:T(8,128)(2,1)S(1)}, u32[]{:S(2)}, u32[]{:S(2)}) collective-permute-start(bf16[128,256]{0,1:T(8,128)(2,1)S(1)} %collective-permute-done.12), channel_id=1, source_target_pairs={{0,4},{4,8},{8,12},{12,16},{16,20},{20,24},{24,28},{28,32},{32,36}... | collective-permute-start | bytes 196616 | tf_op jit(solution)/shard_map/ppermute | solution.py:25
  68.4 16.3 %copy-start.15 = (bf16[128,256]{0,1:T(8,128)(2,1)}, bf16[128,256]{0,1:T(8,128)(2,1)S(1)}, u32[]{:S(2)}) copy-start(bf16[128,256]{0,1:T(8,128)(2,1)S(1)} %collective-permute-done.6) | copy-start | bytes 196612
  68.4 14.5 %collective-permute-start.7 = (bf16[128,256]{0,1:T(8,128)(2,1)S(1)}, bf16[128,256]{0,1:T(8,128)(2,1)S(1)}, u32[]{:S(2)}, u32[]{:S(2)}) collective-permute-start(bf16[128,256]{0,1:T(8,128)(2,1)S(1)} %collective-permute-done.6), channel_id=1, source_target_pairs={{0,60},{4,0},{8,4},{12,8},{16,12},{20,16},{24,20},{28,24},{32,28},... | collective-permute-start | bytes 196616 | tf_op jit(solution)/shard_map/ppermute | solution.py:25
  73.5 11.1 %copy-start.13 = (bf16[128,256]{0,1:T(8,128)(2,1)}, bf16[128,256]{0,1:T(8,128)(2,1)S(1)}, u32[]{:S(2)}) copy-start(bf16[128,256]{0,1:T(8,128)(2,1)S(1)} %collective-permute-done.13) | copy-start | bytes 196612
  73.5 7.5 %collective-permute-start.14 = (bf16[128,256]{0,1:T(8,128)(2,1)S(1)}, bf16[128,256]{0,1:T(8,128)(2,1)}, u32[]{:S(2)}, u32[]{:S(2)}) collective-permute-start(bf16[128,256]{0,1:T(8,128)(2,1)S(1)} %collective-permute-done.13), channel_id=1, source_target_pairs={{0,4},{4,8},{8,12},{12,16},{16,20},{20,24},{24,28},{28,32},{32,36}... | collective-permute-start | bytes 196616 | tf_op jit(solution)/shard_map/ppermute | solution.py:25
  81.0 14.8 %collective-permute-start.15 = (bf16[128,256]{0,1:T(8,128)(2,1)}, bf16[128,256]{0,1:T(8,128)(2,1)}, u32[]{:S(2)}, u32[]{:S(2)}) collective-permute-start(bf16[128,256]{0,1:T(8,128)(2,1)} %collective-permute-done.14), channel_id=1, source_target_pairs={{0,4},{4,8},{8,12},{12,16},{16,20},{20,24},{24,28},{28,32},{32,36}... | collective-permute-start | bytes 196616 | tf_op jit(solution)/shard_map/ppermute | solution.py:25
  88.2 11.7 %copy-start.4 = (bf16[128,256]{0,1:T(8,128)(2,1)S(1)}, bf16[128,256]{0,1:T(8,128)(2,1)}, u32[]{:S(2)}) copy-start(bf16[128,256]{0,1:T(8,128)(2,1)} %copy-done.3) | copy-start | bytes 196612
  89.8 14.5 %copy-start.6 = (bf16[128,256]{0,1:T(8,128)(2,1)S(1)}, bf16[128,256]{0,1:T(8,128)(2,1)}, u32[]{:S(2)}) copy-start(bf16[128,256]{0,1:T(8,128)(2,1)} %copy-done.5) | copy-start | bytes 196612
  89.8 15.2 %copy-start.8 = (bf16[128,256]{0,1:T(8,128)(2,1)S(1)}, bf16[128,256]{0,1:T(8,128)(2,1)}, u32[]{:S(2)}) copy-start(bf16[128,256]{0,1:T(8,128)(2,1)} %copy-done.7) | copy-start | bytes 196612
  89.8 15.8 %copy-start.12 = (bf16[128,256]{0,1:T(8,128)(2,1)S(1)}, bf16[128,256]{0,1:T(8,128)(2,1)}, u32[]{:S(2)}) copy-start(bf16[128,256]{0,1:T(8,128)(2,1)} %copy-done.11) | copy-start | bytes 196612
  89.8 16.4 %copy-start.16 = (bf16[128,256]{0,1:T(8,128)(2,1)S(1)}, bf16[128,256]{0,1:T(8,128)(2,1)}, u32[]{:S(2)}) copy-start(bf16[128,256]{0,1:T(8,128)(2,1)} %copy-done.15) | copy-start | bytes 196612
  89.8 17.0 %copy-start.18 = (bf16[128,256]{0,1:T(8,128)(2,1)S(1)}, bf16[128,256]{0,1:T(8,128)(2,1)}, u32[]{:S(2)}) copy-start(bf16[128,256]{0,1:T(8,128)(2,1)} %copy-done.17) | copy-start | bytes 196612
  89.8 55.9 %all-to-all-start = ((bf16[16,272,128]{2,1,0:T(8,128)(2,1)}), bf16[16,272,128]{2,1,0:T(8,128)(2,1)S(1)}, u32[]{:S(2)}, u32[]{:S(2)}) async-start(bf16[16,272,128]{2,1,0:T(8,128)(2,1)} %copy.59), calls=%async_computation | async-start | bytes 2228224 | tf_op jit(solution)/shard_map/all_to_all | solution.py:131
  (6 other events, 28.1 us)

commit v3 on v1

v3 whole, which is shorter than its diff:
```python
import jax
import jax.numpy as jnp
from jax import lax
from jax.sharding import Mesh
from jax.sharding import PartitionSpec as P

BLEND_CHANNELS = 128
P_SIZE = 64
N = 128
GROUPS = 4
MISC = 16
LOCAL = 4

F32 = jnp.float32
BF16 = jnp.bfloat16
HIGH = lax.Precision.HIGHEST
SEQ = ("hi", "lo")


def from_behind(value, axis, steps):
    count = lax.axis_size(axis)
    leading, last = (max(0, -steps), min(count, count - steps))
    return lax.ppermute(value, axis, [(source, source + steps) for source in range(leading, last)])


def mm(spec, a, b):
    return jnp.einsum(spec, a, b, preferred_element_type=F32)


def mm_wide(spec, a, b):
    return jnp.einsum(spec, a.astype(F32), b.astype(F32), precision=HIGH)


def local_terms(xk, gk, bk, ck, deck, flk):
    chunks, width = flk.shape
    order = jnp.arange(width)
    causal = order[:, None] >= order[None, :]
    tri = causal.astype(BF16)
    cum = mm("tu,khu->kht", tri, deck)
    seg = mm("tu,ku->kt", tri, flk)

    cum_end = cum[:, :, -1]
    seg_end = seg[:, -1]
    outflow = jnp.exp(cum_end[:, :, None] - cum) * (seg == seg_end[:, None])[:, None, :]
    inflow = jnp.exp(cum) * (seg == 0.0)[:, None, :]
    outflow_q = outflow.transpose(0, 2, 1)[..., None]
    inflow_q = inflow.transpose(0, 2, 1)[..., None]
    end_states = mm_wide("kun,kuhp->khnp", bk, outflow_q * xk.astype(F32))
    start_states = mm_wide("ktn,kthp->khnp", ck, inflow_q * gk.astype(F32))

    total = jnp.cumsum(cum_end, axis=0)
    opened = jnp.cumsum((seg_end > 0.0).astype(F32))
    total_prev = jnp.concatenate([jnp.zeros_like(total[:1]), total[:-1]], axis=0)
    opened_prev = jnp.concatenate([jnp.zeros_like(opened[:1]), opened[:-1]], axis=0)
    index = jnp.arange(chunks)
    reach = (index[None, :] < index[:, None]) & (opened_prev[:, None] == opened[None, :])
    carry = jnp.where(
        reach[:, :, None],
        jnp.exp(jnp.minimum(total_prev[:, None, :] - total[None, :, :], 0.0)),
        0.0,
    )
    from_start = jnp.exp(total_prev) * (opened_prev == 0.0)[:, None]
    to_end = jnp.exp(jnp.minimum(total[-1][None, :] - total, 0.0)) * (opened == opened[-1])[:, None]
    through = jnp.exp(total[-1]) * (opened[-1] == 0.0)
    block_end = jnp.einsum("kh,khnp->hnp", to_end, end_states, precision=HIGH)
    block_start = jnp.einsum("kh,khnp->hnp", from_start, start_states, precision=HIGH)
    parts = dict(
        cum=cum, seg=seg, causal=causal, inflow_q=inflow_q, outflow_q=outflow_q,
        end_states=end_states, start_states=start_states, carry=carry,
        from_start=from_start, to_end=to_end,
    )
    return parts, through, block_end, block_start


def finish(parts, xk, gk, bk, ck, gain, entering_block, leaving_block):
    cum, seg, causal = parts["cum"], parts["seg"], parts["causal"]
    linked = (seg[:, :, None] == seg[:, None, :]) & causal[None]
    spread = cum[:, :, :, None] - cum[:, :, None, :]
    damping = jnp.where(linked[:, None], jnp.exp(jnp.minimum(spread, 0.0)), 0.0)
    overlap = mm("ktn,kun->ktu", ck, bk)
    mixing = damping * overlap[:, None]
    mixed = mm_wide("khtu,kuhp->kthp", mixing, xk)
    grads = mm_wide("khtu,kthp->kuhp", mixing, gk)

    carry = parts["carry"]
    entering = jnp.einsum("kjh,jhnp->khnp", carry, parts["end_states"], precision=HIGH)
    leaving = jnp.einsum("jkh,jhnp->khnp", carry, parts["start_states"], precision=HIGH)
    entering = entering + parts["from_start"][:, :, None, None] * entering_block[None]
    leaving = leaving + parts["to_end"][:, :, None, None] * leaving_block[None]

    mixed = mixed + parts["inflow_q"] * mm_wide("ktn,khnp->kthp", ck, entering)
    grads = grads + parts["outflow_q"] * mm_wide("kun,khnp->kuhp", bk, leaving)
    gain_wide = gain[None, None, :, None]
    mixed = mixed + gain_wide * xk.astype(F32)
    grads = grads + gain_wide * gk.astype(F32)
    return mixed, grads


def body(emitted, cotangent, b_proj, c_proj, log_decay, starts, skip):
    shifted = from_behind(emitted, "pipe", 1)
    inputs = jnp.where(lax.axis_index("pipe") == 0, emitted, shifted)[0]
    upstream = cotangent[0]
    length_dev = inputs.shape[0]
    lo_count = lax.axis_size("lo")
    hi_count = lax.axis_size("hi")
    local_heads = skip.shape[1]
    head_share = local_heads // lo_count
    lanes = head_share * P_SIZE
    rows = lanes * length_dev // 128
    lo_pos = lax.axis_index("lo")
    first_head = lo_pos * head_share

    def to_rows(value):
        return value.reshape(length_dev, lo_count, lanes).transpose(1, 0, 2).reshape(lo_count, rows, 128)

    decay_rows = log_decay[0].reshape(length_dev, lo_count, head_share).transpose(1, 2, 0)
    flag_rows = jnp.broadcast_to(starts[0].astype(BF16)[None, None, :], (lo_count, 1, length_dev))
    proj = jnp.concatenate([b_proj[0], c_proj[0]], axis=0)
    proj_rows = jnp.broadcast_to(proj[None], (lo_count,) + proj.shape)
    filler = jnp.zeros((lo_count, MISC - head_share - 1, length_dev), BF16)
    payload = jnp.concatenate(
        [to_rows(inputs), to_rows(upstream), proj_rows, decay_rows, flag_rows, filler], axis=1
    )
    got = lax.all_to_all(payload, "lo", split_axis=0, concat_axis=0, tiled=True)

    xk = got[:, :rows].reshape(lo_count, length_dev, head_share, P_SIZE)
    gk = got[:, rows : 2 * rows].reshape(lo_count, length_dev, head_share, P_SIZE)
    base = 2 * rows
    bk = got[:, base : base + length_dev]
    ck = got[:, base + length_dev : base + 2 * length_dev]
    base = base + 2 * length_dev
    deck = got[:, base : base + head_share]
    flk = got[:, base + head_share]
    gain = lax.dynamic_slice_in_dim(skip[0], first_head, head_share)

    parts, through, block_end, block_start = local_terms(xk, gk, bk, ck, deck, flk)

    entering_block = jnp.zeros_like(block_end)
    leaving_block = jnp.zeros_like(block_start)
    for _ in range(hi_count - 1):
        entering_block = from_behind(through[:, None, None] * entering_block + block_end, "hi", 1)
        leaving_block = from_behind(through[:, None, None] * leaving_block + block_start, "hi", -1)

    mixed, grads = finish(parts, xk, gk, bk, ck, gain, entering_block, leaving_block)
    homeward = jnp.concatenate(
        [mixed.reshape(lo_count, rows, 128), grads.reshape(lo_count, rows, 128)], axis=1
    ).astype(BF16)
    back = lax.all_to_all(homeward, "lo", split_axis=0, concat_axis=0, tiled=True)

    def from_rows(value):
        return value.reshape(lo_count, length_dev, lanes).transpose(1, 0, 2).reshape(
            1, length_dev, local_heads * P_SIZE
        )

    return (from_rows(back[:, :rows]), from_rows(back[:, rows:]))


def solution(mesh):
    pipe_count, seq_count, tp_count = mesh.devices.shape
    split_mesh = Mesh(
        mesh.devices.reshape(pipe_count, seq_count // LOCAL, LOCAL, tp_count),
        ("pipe", "hi", "lo", "tp"),
    )
    placed = (
        P("pipe", SEQ, "tp"),
        P("pipe", SEQ, "tp"),
        P("pipe", SEQ, "tp"),
        P("pipe", SEQ, "tp"),
        P("pipe", SEQ, "tp"),
        P("pipe", SEQ),
        P("pipe", "tp"),
    )
    return jax.shard_map(
        body,
        mesh=split_mesh,
        in_specs=placed,
        out_specs=(P("pipe", SEQ, "tp"), P("pipe", SEQ, "tp")),
        check_vma=False,
    )
```

time: 224 us -> 214 us (0.955)
  the two profiles are of different devices: /device:TPU:92 before, /device:TPU:16 now
where the time goes in v3:
time: 214 us; the launch traced here: 213 us
  starting transfers between devices  58.7 us (27%)
  waiting for transfers between devices  56 us (26%)
  blocking collectives  49 us (23%)
  local copies, waits for them, and re-layouts  24.5 us (11%)
  matrix products  16.1 us (8%)
  other arithmetic  7.06 us (3%)
    ppermute x7, starting transfers between devices, from_behind(): lax.ppermute(value, axis, [(source, source + steps) for source in range(l...  51.5 us
    all_to_all x1, blocking collectives, body(): lax.all_to_all(homeward, 'lo', split_axis=0, concat_axis=0, tiled=True)  49 us
    all_to_all x1, waiting for transfers between devices, body(): got = lax.all_to_all(payload, 'lo', split_axis=0, concat_axis=0, tiled=True)  29.9 us
    ppermute x7, waiting for transfers between devices, from_behind(): lax.ppermute(value, axis, [(source, source + steps) for source in range(l...  26 us
    all_to_all x1, starting transfers between devices, body(): got = lax.all_to_all(payload, 'lo', split_axis=0, concat_axis=0, tiled=True)  7.26 us
    dot_general x4, matrix products, mm_wide(): return jnp.einsum(spec, a.astype(F32), b.astype(F32), precision=HIGH)  6.57 us
    concatenate x1, local copies, waits for them, and re-layouts, body(): jnp.concatenate([to_rows(inputs), to_rows(upstream), proj_rows, decay_row...  4.83 us
  transfers between devices with their start and end apart: 8, of which 6 were waited for; matrix products, arithmetic and copies ran while one was open for 10% of the time, Pallas kernels for 0%

profile of v3, /device:TPU:16, one launch (start us, length us, event | category | flops | bytes accessed | tf_op | source)
XLA Modules:
  0.0 213.2 jit_solution(2992988182670370590)
XLA Ops:
  0.6 1.9 collective-permute-start
  2.6 1.4 reshape_squeeze.10
  4.7 6.6 %collective-permute-done = bf16[1,128,2048]{2,1,0:T(8,128)(2,1)S(1)} collective-permute-done((bf16[1,128,2048]{2,1,0:T(8,128)(2,1)}, bf16[1,128,2048]{2,1,0:T(8,128)(2,1)S(1)}, u32[]{:S(2)}, u32[]{:S(2)}) %collective-permute-start) | collective-permute-done | bytes 524320 | tf_op jit(solution)/shard_map/ppermute | solution.py:23
  12.5 4.8 %concatenate.21 = bf16[4,1296,128]{2,1,0:T(8,128)(2,1)} concatenate(bf16[4,512,128]{2,1,0:T(8,128)(2,1)S(1)} %reshape.186, bf16[4,512,128]{2,1,0:T(8,128)(2,1)S(1)} %reshape.187, bf16[4,256,128]{2,1,0:T(8,128)(2,1)S(1)} %broadcast_in_dim.18, bf16[4,8,128]{2,1,0:T(8,128)(2,1)S(1)} %bitcast.137, bf16[4,1,128]{2,1,0:T(2,128)(2,1)S(1)} %broadcast_in_dim.19, ...), dimensions={1} | concatenate | bytes 2654208 | tf_op jit(solution)/shard_map/concatenate | solution.py:121
  17.3 7.3 %all-to-all-start = ((bf16[4,1296,128]{2,1,0:T(8,128)(2,1)}), bf16[4,1296,128]{2,1,0:T(8,128)(2,1)S(1)}, u32[]{:S(2)}, u32[]{:S(2)}) async-start(bf16[4,1296,128]{2,1,0:T(8,128)(2,1)} %concatenate.21), calls=%async_computation | async-start | bytes 2654208 | tf_op jit(solution)/shard_map/all_to_all | solution.py:124
  25.8 29.9 %all-to-all-done = bf16[4,1296,128]{2,1,0:T(8,128)(2,1)S(1)} async-done(((bf16[4,1296,128]{2,1,0:T(8,128)(2,1)}), bf16[4,1296,128]{2,1,0:T(8,128)(2,1)S(1)}, u32[]{:S(2)}, u32[]{:S(2)}) %all-to-all-start) | async-done | bytes 1327136 | tf_op jit(solution)/shard_map/all_to_all | solution.py:124
  60.3 1.4 copy.25
  63.5 10.9 %collective-permute-start.1 = (f32[8,128,64]{1,2,0:T(8,128)S(1)}, f32[8,128,64]{1,2,0:T(8,128)S(1)}, u32[]{:S(2)}, u32[]{:S(2)}) collective-permute-start(f32[8,128,64]{1,2,0:T(8,128)S(1)} %get-tuple-element.16), channel_id=1, source_target_pairs={{0,16},{16,32},{32,48},{1,17},{17,33},{33,49},{2,18},{18,34},{34,5... | collective-permute-start | bytes 786440 | tf_op jit(solution)/shard_map/ppermute | solution.py:23
  75.1 1.3 collective-permute-start.4
  76.6 2.8 %collective-permute-done.1 = f32[8,128,64]{1,2,0:T(8,128)S(1)} collective-permute-done((f32[8,128,64]{1,2,0:T(8,128)S(1)}, f32[8,128,64]{1,2,0:T(8,128)S(1)}, u32[]{:S(2)}, u32[]{:S(2)}) %collective-permute-start.1) | collective-permute-done | bytes 262176 | tf_op jit(solution)/shard_map/ppermute | solution.py:23
  79.4 15.0 %collective-permute-start.2 = (f32[8,128,64]{1,2,0:T(8,128)S(1)}, f32[8,128,64]{1,2,0:T(8,128)S(1)}, u32[]{:S(2)}, u32[]{:S(2)}) collective-permute-start(f32[8,128,64]{1,2,0:T(8,128)S(1)} %multiply_add_fusion.5), channel_id=1, source_target_pairs={{0,16},{16,32},{32,48},{1,17},{17,33},{33,49},{2,18},{18,34},{34,5... | collective-permute-start | bytes 786440 | tf_op jit(solution)/shard_map/ppermute | solution.py:23
  95.1 0.9 fusion.33
  96.0 9.5 %collective-permute-done.4 = f32[8,128,64]{1,2,0:T(8,128)S(1)} collective-permute-done((f32[8,128,64]{1,2,0:T(8,128)S(1)}, f32[8,128,64]{1,2,0:T(8,128)S(1)}, u32[]{:S(2)}, u32[]{:S(2)}) %collective-permute-start.4) | collective-permute-done | bytes 262176 | tf_op jit(solution)/shard_map/ppermute | solution.py:23
  105.5 0.9 multiply_add_fusion.4
  106.5 1.3 collective-permute-start.5
  107.8 19.6 %collective-permute-start.3 = (f32[8,128,64]{1,2,0:T(8,128)}, f32[8,128,64]{1,2,0:T(8,128)}, u32[]{:S(2)}, u32[]{:S(2)}) collective-permute-start(f32[8,128,64]{1,2,0:T(8,128)} %get-tuple-element.14), channel_id=1, source_target_pairs={{0,16},{16,32},{32,48},{1,17},{17,33},{33,49},{2,18},{18,34},{34,5... | collective-permute-start | bytes 786440 | tf_op jit(solution)/shard_map/ppermute | solution.py:23
  128.7 0.8 copy.37
  129.5 0.8 concatenate.23.clone
  130.2 1.3 copy.31
  131.6 2.4 %collective-permute-done.5 = f32[8,128,64]{1,2,0:T(8,128)} collective-permute-done((f32[8,128,64]{1,2,0:T(8,128)}, f32[8,128,64]{1,2,0:T(8,128)}, u32[]{:S(2)}, u32[]{:S(2)}) %collective-permute-start.5) | collective-permute-done | bytes 262176 | tf_op jit(solution)/shard_map/ppermute | solution.py:23
  133.9 1.8 multiply_add_fusion.2
  135.7 1.5 collective-permute-start.6
  137.2 3.6 %multiply_add_fusion.1 = f32[4,8,128,64]{2,0,3,1:T(4,128)S(1)} fusion(f32[8,128,64]{1,2,0:T(8,128)} %collective-permute-done.3, f32[4,8]{0,1:T(8,128)} %copy.31, f32[4,8,128,64]{2,3,1,0:T(8,128)S(1)} %bitcast.123, f32[4,8]{0,1:T(8,128)S(1)} %copy.28, f32[4,8]{0,1:T(8,128)S(1)} %concatenate.23.clone, pred[4,4]{0,1:T(4,128)(4,1)} %fusion.61), kind=kOutput, calls=%fused_computation.27 | convolution fusion | flops 13107584 | bytes 2359696 | tf_op jit(solution)/shard_map/kjh,jhnp->khnp/dot_general | solution.py:86
  142.1 3.3 %fusion.9 = bf16[4,128,8,64]{1,3,2,0:T(8,128)(2,1)} fusion(bf16[4,128,8,64]{1,3,2,0:T(8,128)(2,1)S(1)} %copy-done.5, f32[4,128,8,64]{1,3,2,0:T(8,128)S(1)} %bitcast.131, f32[4,128,128]{2,1,0:T(8,128)S(1)} %copy-done.8, f32[4,8,128]{2,1,0:T(8,128)S(1)} %fusion.39, pred[4,128,128]{2,1,0:T(8,128)(4,1)S(1)} %compare_and_fusion, f32[8]{0:T(128)S(1)} %copy-done.19, ...), kind=kOutput, calls=%fused_computation.16 | convolution fusion | flops 406323200 | bytes 2457632 | tf_op jit(solution)/shard_map/khtu,kuhp->kthp/dot_general | solution.py:31
  145.4 1.6 copy.33
  147.0 1.3 reshape.189
  148.3 4.8 %collective-permute-done.6 = f32[8,128,64]{1,2,0:T(8,128)} collective-permute-done((f32[8,128,64]{1,2,0:T(8,128)}, f32[8,128,64]{1,2,0:T(8,128)}, u32[]{:S(2)}, u32[]{:S(2)}) %collective-permute-start.6) | collective-permute-done | bytes 262176 | tf_op jit(solution)/shard_map/ppermute | solution.py:23
  153.0 3.5 %multiply_add_fusion = f32[4,8,128,64]{2,0,3,1:T(4,128)S(1)} fusion(f32[8,128,64]{1,2,0:T(8,128)} %collective-permute-done.6, f32[4,8]{0,1:T(8,128)S(1)} %copy.37, f32[4,8,128,64]{2,3,1,0:T(8,128)S(1)} %bitcast.122, f32[4,8]{0,1:T(8,128)S(1)} %copy.28, f32[4,8]{0,1:T(8,128)S(1)} %concatenate.23.clone, pred[4,4]{0,1:T(4,128)(4,1)S(1)} %copy-done.15), kind=kOutput, calls=%fused_computation.26 | convolution fusion | flops 13107584 | bytes 2359696 | tf_op jit(solution)/shard_map/jkh,jhnp->khnp/dot_general | solution.py:87
  157.8 1.9 fusion.8
  160.9 49.0 %all_to_all.10 = bf16[4,1024,128]{2,1,0:T(8,128)(2,1)S(1)} all-to-all(bf16[4,1024,128]{2,1,0:T(8,128)(2,1)S(1)} %pad_maximum_fusion), channel_id=1, replica_groups=mesh['pipe'=16,'hi'=4,'lo'=4,'tp'=4] {'lo'}, dimensions={0} | all-to-all | bytes 2097152 | tf_op jit(solution)/shard_map/all_to_all | solution.py:148
  210.6 1.0 copy.42
  212.2 1.0 copy.43
  (103 shorter events, 16.3 us)
Async XLA Ops:
  0.6 24.0 %copy-start = (f32[1,32]{1,0:T(1,128)S(1)}, f32[1,32]{1,0:T(1,128)}, u32[]{:S(2)}) copy-start(f32[1,32]{1,0:T(1,128)} %param.13) | copy-start | bytes 388
  0.6 10.7 %collective-permute-start = (bf16[1,128,2048]{2,1,0:T(8,128)(2,1)}, bf16[1,128,2048]{2,1,0:T(8,128)(2,1)S(1)}, u32[]{:S(2)}, u32[]{:S(2)}) collective-permute-start(bf16[1,128,2048]{2,1,0:T(8,128)(2,1)} %param.7), channel_id=1, source_target_pairs={{0,64},{64,128},{128,192},{192,256},{256,320},{320,384},{384,448},... | collective-permute-start | bytes 1572872 | tf_op jit(solution)/shard_map/ppermute | solution.py:23
  2.6 1.9 copy-start.11
  2.6 1.9 copy-start.12
  4.0 0.7 copy-start.18
  4.1 7.3 %copy-start.7 = (bf16[1,128,2048]{2,1,0:T(8,128)(2,1)S(1)}, bf16[1,128,2048]{2,1,0:T(8,128)(2,1)}, u32[]{:S(2)}) copy-start(bf16[1,128,2048]{2,1,0:T(8,128)(2,1)} %param.7) | copy-start | bytes 1572868
  11.8 0.7 copy-start.13
  17.3 38.4 %all-to-all-start = ((bf16[4,1296,128]{2,1,0:T(8,128)(2,1)}), bf16[4,1296,128]{2,1,0:T(8,128)(2,1)S(1)}, u32[]{:S(2)}, u32[]{:S(2)}) async-start(bf16[4,1296,128]{2,1,0:T(8,128)(2,1)} %concatenate.21), calls=%async_computation | async-start | bytes 2654208 | tf_op jit(solution)/shard_map/all_to_all | solution.py:124
  58.0 4.0 %copy-start.2 = (bf16[4,128,8,64]{1,3,2,0:T(8,128)(2,1)}, bf16[4,128,8,64]{1,3,2,0:T(8,128)(2,1)S(1)}, u32[]{:S(2)}) copy-start(bf16[4,128,8,64]{1,3,2,0:T(8,128)(2,1)S(1)} %copy.34) | copy-start | bytes 1572868
  58.5 3.1 %copy-start.16 = (f32[4]{0:T(128)}, f32[4]{0:T(128)S(1)}, u32[]{:S(2)}) copy-start(f32[4]{0:T(128)S(1)} %reduce.5) | copy-start | bytes 52
  61.7 1.0 copy-start.4
  61.7 43.8 %copy-start.14 = (f32[8]{0:T(128)}, f32[8]{0:T(128)S(1)}, u32[]{:S(2)}) copy-start(f32[8]{0:T(128)S(1)} %get-tuple-element.5) | copy-start | bytes 100
  62.7 42.8 %copy-start.1 = (f32[8,128,64]{1,2,0:T(8,128)}, f32[8,128,64]{1,2,0:T(8,128)S(1)}, u32[]{:S(2)}) copy-start(f32[8,128,64]{1,2,0:T(8,128)S(1)} %get-tuple-element.18) | copy-start | bytes 786436
  62.7 13.7 %copy-start.10 = (pred[128,128]{1,0:T(8,128)(4,1)S(1)}, pred[128,128]{1,0:T(8,128)(4,1)}, u32[]{:S(2)}) copy-start(pred[128,128]{1,0:T(8,128)(4,1)} %iota_compare_fusion) | copy-start | bytes 49156
  63.5 15.8 %collective-permute-start.1 = (f32[8,128,64]{1,2,0:T(8,128)S(1)}, f32[8,128,64]{1,2,0:T(8,128)S(1)}, u32[]{:S(2)}, u32[]{:S(2)}) collective-permute-start(f32[8,128,64]{1,2,0:T(8,128)S(1)} %get-tuple-element.16), channel_id=1, source_target_pairs={{0,16},{16,32},{32,48},{1,17},{17,33},{33,49},{2,18},{18,34},{34,5... | collective-permute-start | bytes 786440 | tf_op jit(solution)/shard_map/ppermute | solution.py:23
  75.1 30.4 %collective-permute-start.4 = (f32[8,128,64]{1,2,0:T(8,128)S(1)}, f32[8,128,64]{1,2,0:T(8,128)S(1)}, u32[]{:S(2)}, u32[]{:S(2)}) collective-permute-start(f32[8,128,64]{1,2,0:T(8,128)S(1)} %get-tuple-element.17), channel_id=1, source_target_pairs={{16,0},{32,16},{48,32},{17,1},{33,17},{49,33},{18,2},{34,18},{50,3... | collective-permute-start | bytes 786440 | tf_op jit(solution)/shard_map/ppermute | solution.py:23
  79.3 48.1 %copy-start.17 = (f32[4]{0:T(128)S(1)}, f32[4]{0:T(128)}, u32[]{:S(2)}) copy-start(f32[4]{0:T(128)} %copy-done.16) | copy-start | bytes 52
  79.4 26.1 %collective-permute-start.2 = (f32[8,128,64]{1,2,0:T(8,128)S(1)}, f32[8,128,64]{1,2,0:T(8,128)S(1)}, u32[]{:S(2)}, u32[]{:S(2)}) collective-permute-start(f32[8,128,64]{1,2,0:T(8,128)S(1)} %multiply_add_fusion.5), channel_id=1, source_target_pairs={{0,16},{16,32},{32,48},{1,17},{17,33},{33,49},{2,18},{18,34},{34,5... | collective-permute-start | bytes 786440 | tf_op jit(solution)/shard_map/ppermute | solution.py:23
  106.5 27.5 %collective-permute-start.5 = (f32[8,128,64]{1,2,0:T(8,128)}, f32[8,128,64]{1,2,0:T(8,128)}, u32[]{:S(2)}, u32[]{:S(2)}) collective-permute-start(f32[8,128,64]{1,2,0:T(8,128)} %get-tuple-element.15), channel_id=1, source_target_pairs={{16,0},{32,16},{48,32},{17,1},{33,17},{49,33},{18,2},{34,18},{50,3... | collective-permute-start | bytes 786440 | tf_op jit(solution)/shard_map/ppermute | solution.py:23
  107.8 29.4 %collective-permute-start.3 = (f32[8,128,64]{1,2,0:T(8,128)}, f32[8,128,64]{1,2,0:T(8,128)}, u32[]{:S(2)}, u32[]{:S(2)}) collective-permute-start(f32[8,128,64]{1,2,0:T(8,128)} %get-tuple-element.14), channel_id=1, source_target_pairs={{0,16},{16,32},{32,48},{1,17},{17,33},{33,49},{2,18},{18,34},{34,5... | collective-permute-start | bytes 786440 | tf_op jit(solution)/shard_map/ppermute | solution.py:23
  135.7 17.3 %collective-permute-start.6 = (f32[8,128,64]{1,2,0:T(8,128)}, f32[8,128,64]{1,2,0:T(8,128)}, u32[]{:S(2)}, u32[]{:S(2)}) collective-permute-start(f32[8,128,64]{1,2,0:T(8,128)} %multiply_add_fusion.2), channel_id=1, source_target_pairs={{16,0},{32,16},{48,32},{17,1},{33,17},{49,33},{18,2},{34,18},{50,3... | collective-permute-start | bytes 786440 | tf_op jit(solution)/shard_map/ppermute | solution.py:23
  141.0 1.0 copy-start.5
  141.0 1.1 copy-start.8
  141.0 1.1 copy-start.19
  145.4 7.6 %copy-start.15 = (pred[4,4]{0,1:T(4,128)(4,1)S(1)}, pred[4,4]{0,1:T(4,128)(4,1)}, u32[]{:S(2)}) copy-start(pred[4,4]{0,1:T(4,128)(4,1)} %fusion.61) | copy-start | bytes 52
  156.7 1.0 copy-start.3
  156.7 1.1 copy-start.9
  156.8 1.1 copy-start.20
  159.7 1.1 copy-start.6

commit v4 on v3

--- a/solution.py
+++ b/solution.py
@@ -10,6 +10,7 @@
 GROUPS = 4
 MISC = 16
 LOCAL = 4
+PIECES = 2
 
 F32 = jnp.float32
 BF16 = jnp.bfloat16
@@ -96,6 +97,19 @@
     return mixed, grads
 
 
+def chain(block, through, count, steps):
+    pieces = []
+    width = block.shape[0] // PIECES
+    for piece in range(PIECES):
+        own = block[piece * width : (piece + 1) * width]
+        gain = through[piece * width : (piece + 1) * width, None, None]
+        state = jnp.zeros_like(own)
+        for _ in range(count - 1):
+            state = from_behind(gain * state + own, "hi", steps)
+        pieces.append(state)
+    return jnp.concatenate(pieces, axis=0)
+
+
 def body(emitted, cotangent, b_proj, c_proj, log_decay, starts, skip):
     shifted = from_behind(emitted, "pipe", 1)
     inputs = jnp.where(lax.axis_index("pipe") == 0, emitted, shifted)[0]
@@ -135,11 +149,8 @@
 
     parts, through, block_end, block_start = local_terms(xk, gk, bk, ck, deck, flk)
 
-    entering_block = jnp.zeros_like(block_end)
-    leaving_block = jnp.zeros_like(block_start)
-    for _ in range(hi_count - 1):
-        entering_block = from_behind(through[:, None, None] * entering_block + block_end, "hi", 1)
-        leaving_block = from_behind(through[:, None, None] * leaving_block + block_start, "hi", -1)
+    entering_block = chain(block_end, through, hi_count, 1)
+    leaving_block = chain(block_start, through, hi_count, -1)
 
     mixed, grads = finish(parts, xk, gk, bk, ck, gain, entering_block, leaving_block)
     homeward = jnp.concatenate(

time: 214 us -> 224 us (1.047)
  the two profiles are of different devices: /device:TPU:16 before, /device:TPU:1 now
where the time goes in v4:
time: 224 us; the launch traced here: 223 us
  waiting for transfers between devices  78.7 us (35%)
  starting transfers between devices  67.9 us (30%)
  blocking collectives  27.3 us (12%)
  local copies, waits for them, and re-layouts  23.2 us (10%)
  matrix products  15.5 us (7%)
  other arithmetic  8.89 us (4%)
    ppermute x13, starting transfers between devices, from_behind(): lax.ppermute(value, axis, [(source, source + steps) for source in range(l...  64.4 us
    ppermute x13, waiting for transfers between devices, from_behind(): lax.ppermute(value, axis, [(source, source + steps) for source in range(l...  48.7 us
    all_to_all x1, waiting for transfers between devices, body(): got = lax.all_to_all(payload, 'lo', split_axis=0, concat_axis=0, tiled=True)  30 us
    all_to_all x1, blocking collectives, body(): lax.all_to_all(homeward, 'lo', split_axis=0, concat_axis=0, tiled=True)  27.3 us
    dot_general x4, matrix products, mm_wide(): return jnp.einsum(spec, a.astype(F32), b.astype(F32), precision=HIGH)  7.7 us
    concatenate x1, local copies, waits for them, and re-layouts, body(): jnp.concatenate([to_rows(inputs), to_rows(upstream), proj_rows, decay_row...  4.79 us
  transfers between devices with their start and end apart: 14, of which 5 were waited for; matrix products, arithmetic and copies ran while one was open for 9% of the time, Pallas kernels for 0%

profile of v4, /device:TPU:1, one launch (start us, length us, event | category | flops | bytes accessed | tf_op | source)
XLA Modules:
  0.0 223.5 jit_solution(9302828924257955870)
XLA Ops:
  0.6 4.6 %collective-permute-start = (bf16[1,128,2048]{2,1,0:T(8,128)(2,1)}, bf16[1,128,2048]{2,1,0:T(8,128)(2,1)S(1)}, u32[]{:S(2)}, u32[]{:S(2)}) collective-permute-start(bf16[1,128,2048]{2,1,0:T(8,128)(2,1)} %param.7), channel_id=1, source_target_pairs={{0,64},{64,128},{128,192},{192,256},{256,320},{320,384},{384,448},... | collective-permute-start | bytes 1572872 | tf_op jit(solution)/shard_map/ppermute | solution.py:24
  5.3 1.4 reshape_squeeze.10
  7.4 10.3 %collective-permute-done = bf16[1,128,2048]{2,1,0:T(8,128)(2,1)S(1)} collective-permute-done((bf16[1,128,2048]{2,1,0:T(8,128)(2,1)}, bf16[1,128,2048]{2,1,0:T(8,128)(2,1)S(1)}, u32[]{:S(2)}, u32[]{:S(2)}) %collective-permute-start) | collective-permute-done | bytes 524320 | tf_op jit(solution)/shard_map/ppermute | solution.py:24
  18.8 4.8 %concatenate.27 = bf16[4,1296,128]{2,1,0:T(8,128)(2,1)} concatenate(bf16[4,512,128]{2,1,0:T(8,128)(2,1)S(1)} %reshape.182, bf16[4,512,128]{2,1,0:T(8,128)(2,1)S(1)} %reshape.183, bf16[4,256,128]{2,1,0:T(8,128)(2,1)S(1)} %broadcast_in_dim.18, bf16[4,8,128]{2,1,0:T(8,128)(2,1)S(1)} %bitcast.136, bf16[4,1,128]{2,1,0:T(2,128)(2,1)S(1)} %broadcast_in_dim.19, ...), dimensions={1} | concatenate | bytes 2654208 | tf_op jit(solution)/shard_map/concatenate | solution.py:135
  23.6 3.5 %all-to-all-start = ((bf16[4,1296,128]{2,1,0:T(8,128)(2,1)}), bf16[4,1296,128]{2,1,0:T(8,128)(2,1)S(1)}, u32[]{:S(2)}, u32[]{:S(2)}) async-start(bf16[4,1296,128]{2,1,0:T(8,128)(2,1)} %concatenate.27), calls=%async_computation | async-start | bytes 2654208 | tf_op jit(solution)/shard_map/all_to_all | solution.py:138
  28.3 30.0 %all-to-all-done = bf16[4,1296,128]{2,1,0:T(8,128)(2,1)S(1)} async-done(((bf16[4,1296,128]{2,1,0:T(8,128)(2,1)}), bf16[4,1296,128]{2,1,0:T(8,128)(2,1)S(1)}, u32[]{:S(2)}, u32[]{:S(2)}) %all-to-all-start) | async-done | bytes 1327136 | tf_op jit(solution)/shard_map/all_to_all | solution.py:138
  59.9 1.4 copy.34
  65.4 1.8 fusion.12
  67.4 1.3 collective-permute-start.7
  68.7 7.9 %collective-permute-start.1 = (f32[4,128,64]{1,2,0:T(8,128)S(1)}, f32[4,128,64]{1,2,0:T(8,128)S(1)}, u32[]{:S(2)}, u32[]{:S(2)}) collective-permute-start(f32[4,128,64]{1,2,0:T(8,128)S(1)} %get-tuple-element.24), channel_id=1, source_target_pairs={{0,16},{16,32},{32,48},{1,17},{17,33},{33,49},{2,18},{18,34},{34,5... | collective-permute-start | bytes 393224 | tf_op jit(solution)/shard_map/ppermute | solution.py:24
  77.6 7.9 %collective-permute-done.7 = f32[4,128,64]{1,2,0:T(8,128)S(1)} collective-permute-done((f32[4,128,64]{1,2,0:T(8,128)S(1)}, f32[4,128,64]{1,2,0:T(8,128)S(1)}, u32[]{:S(2)}, u32[]{:S(2)}) %collective-permute-start.7) | collective-permute-done | bytes 131104 | tf_op jit(solution)/shard_map/ppermute | solution.py:24
  85.6 1.3 collective-permute-start.8
  86.9 1.3 collective-permute-start.10
  88.2 8.5 %collective-permute-start.4 = (f32[4,128,64]{1,2,0:T(8,128)S(1)}, f32[4,128,64]{1,2,0:T(8,128)S(1)}, u32[]{:S(2)}, u32[]{:S(2)}) collective-permute-start(f32[4,128,64]{1,2,0:T(8,128)S(1)} %get-tuple-element.20), channel_id=1, source_target_pairs={{0,16},{16,32},{32,48},{1,17},{17,33},{33,49},{2,18},{18,34},{34,5... | collective-permute-start | bytes 393224 | tf_op jit(solution)/shard_map/ppermute | solution.py:24
  96.8 7.3 %collective-permute-start.2 = (f32[4,128,64]{1,2,0:T(8,128)S(1)}, f32[4,128,64]{1,2,0:T(8,128)S(1)}, u32[]{:S(2)}, u32[]{:S(2)}) collective-permute-start(f32[4,128,64]{1,2,0:T(8,128)S(1)} %get-tuple-element.21), channel_id=1, source_target_pairs={{0,16},{16,32},{32,48},{1,17},{17,33},{33,49},{2,18},{18,34},{34,5... | collective-permute-start | bytes 393224 | tf_op jit(solution)/shard_map/ppermute | solution.py:24
  104.7 4.1 %collective-permute-done.10 = f32[4,128,64]{1,2,0:T(8,128)S(1)} collective-permute-done((f32[4,128,64]{1,2,0:T(8,128)S(1)}, f32[4,128,64]{1,2,0:T(8,128)S(1)}, u32[]{:S(2)}, u32[]{:S(2)}) %collective-permute-start.10) | collective-permute-done | bytes 131104 | tf_op jit(solution)/shard_map/ppermute | solution.py:24
  109.7 9.1 %collective-permute-start.5 = (f32[4,128,64]{1,2,0:T(8,128)}, f32[4,128,64]{1,2,0:T(8,128)}, u32[]{:S(2)}, u32[]{:S(2)}) collective-permute-start(f32[4,128,64]{1,2,0:T(8,128)} %get-tuple-element.22), channel_id=1, source_target_pairs={{0,16},{16,32},{32,48},{1,17},{17,33},{33,49},{2,18},{18,34},{34,5... | collective-permute-start | bytes 393224 | tf_op jit(solution)/shard_map/ppermute | solution.py:24
  118.8 1.3 collective-permute-start.11
  120.9 1.3 copy.37
  123.8 1.3 collective-permute-start.9
  125.1 26.5 %collective-permute-done.11 = f32[4,128,64]{1,2,0:T(8,128)} collective-permute-done((f32[4,128,64]{1,2,0:T(8,128)}, f32[4,128,64]{1,2,0:T(8,128)}, u32[]{:S(2)}, u32[]{:S(2)}) %collective-permute-start.11) | collective-permute-done | bytes 131104 | tf_op jit(solution)/shard_map/ppermute | solution.py:24
  151.5 1.8 multiply_add_fusion.6
  153.4 1.3 collective-permute-start.12
  155.4 12.0 %collective-permute-start.3 = (f32[4,128,64]{1,2,0:T(8,128)}, f32[4,128,64]{1,2,0:T(8,128)}, u32[]{:S(2)}, u32[]{:S(2)}) collective-permute-start(f32[4,128,64]{1,2,0:T(8,128)} %get-tuple-element.23), channel_id=1, source_target_pairs={{0,16},{16,32},{32,48},{1,17},{17,33},{33,49},{2,18},{18,34},{34,5... | collective-permute-start | bytes 393224 | tf_op jit(solution)/shard_map/ppermute | solution.py:24
  167.4 7.3 %collective-permute-start.6 = (f32[4,128,64]{1,2,0:T(8,128)}, f32[4,128,64]{1,2,0:T(8,128)}, u32[]{:S(2)}, u32[]{:S(2)}) collective-permute-start(f32[4,128,64]{1,2,0:T(8,128)} %get-tuple-element.26), channel_id=1, source_target_pairs={{0,16},{16,32},{32,48},{1,17},{17,33},{33,49},{2,18},{18,34},{34,5... | collective-permute-start | bytes 393224 | tf_op jit(solution)/shard_map/ppermute | solution.py:24
  174.7 2.7 %multiply_add_fusion = f32[4,8,128,64]{2,0,3,1:T(4,128)S(1)} fusion(f32[8,128,64]{1,2,0:T(8,128)S(1)} %pad_maximum_fusion.2, f32[4,8]{0,1:T(8,128)S(1)} %copy-done.13, f32[4,8,128,64]{2,3,1,0:T(8,128)S(1)} %bitcast.122, f32[4,8]{0,1:T(8,128)S(1)} %copy.28, f32[4,8]{0,1:T(8,128)S(1)} %concatenate.29.clone, pred[4,4]{0,1:T(4,128)(4,1)S(1)} %fusion.61), kind=kOutput, calls=%fused_computation.26 | convolution fusion | flops 13107584 | bytes 2359696 | tf_op jit(solution)/shard_map/jkh,jhnp->khnp/dot_general | solution.py:88
  178.6 2.6 %fusion.8 = bf16[4,128,8,64]{1,3,2,0:T(8,128)(2,1)} fusion(bf16[4,128,8,64]{1,3,2,0:T(8,128)(2,1)S(1)} %copy-done.5, f32[4,128,8,64]{1,3,2,0:T(8,128)S(1)} %bitcast.130, f32[4,128,128]{2,1,0:T(8,128)S(1)} %copy-done.8, f32[4,8,128]{2,1,0:T(8,128)S(1)} %fusion.39, pred[4,128,128]{2,1,0:T(8,128)(4,1)S(1)} %compare_and_fusion, f32[8]{0:T(128)S(1)} %copy-done.23, ...), kind=kOutput, calls=%fused_computation.15 | convolution fusion | flops 406323200 | bytes 2457632 | tf_op jit(solution)/shard_map/khtu,kthp->kuhp/dot_general | solution.py:32
  181.2 1.6 copy.39
  182.8 1.3 reshape.187
  185.1 2.7 %multiply_add_fusion.1 = f32[4,8,128,64]{2,0,3,1:T(4,128)S(1)} fusion(f32[8,128,64]{1,2,0:T(8,128)S(1)} %pad_maximum_fusion.1, f32[4,8]{0,1:T(8,128)S(1)} %copy.31, f32[4,8,128,64]{2,3,1,0:T(8,128)S(1)} %bitcast.121, f32[4,8]{0,1:T(8,128)S(1)} %copy.28, f32[4,8]{0,1:T(8,128)S(1)} %concatenate.29.clone, pred[4,4]{0,1:T(4,128)(4,1)S(1)} %copy-done.19), kind=kOutput, calls=%fused_computation.27 | convolution fusion | flops 13107584 | bytes 2359696 | tf_op jit(solution)/shard_map/kjh,jhnp->khnp/dot_general | solution.py:87
  189.0 2.6 %fusion.9 = bf16[4,128,8,64]{1,3,2,0:T(8,128)(2,1)S(1)} fusion(bf16[4,128,8,64]{1,3,2,0:T(8,128)(2,1)S(1)} %copy-done.4, f32[4,128,8,64]{1,3,2,0:T(8,128)S(1)} %bitcast.129, f32[4,128,128]{2,1,0:T(8,128)S(1)} %copy-done.9, f32[4,8,128]{2,1,0:T(8,128)S(1)} %fusion.39, pred[4,128,128]{2,1,0:T(8,128)(4,1)S(1)} %compare_and_fusion, f32[8]{0:T(128)S(1)} %copy-done.24, ...), kind=kOutput, calls=%fused_computation.16 | convolution fusion | flops 406323200 | bytes 2457632 | tf_op jit(solution)/shard_map/khtu,kuhp->kthp/dot_general | solution.py:32
  192.8 27.3 %all_to_all.10 = bf16[4,1024,128]{2,1,0:T(8,128)(2,1)S(1)} all-to-all(bf16[4,1024,128]{2,1,0:T(8,128)(2,1)S(1)} %pad_maximum_fusion), channel_id=1, replica_groups=mesh['pipe'=16,'hi'=4,'lo'=4,'tp'=4] {'lo'}, dimensions={0} | all-to-all | bytes 2097152 | tf_op jit(solution)/shard_map/all_to_all | solution.py:159
  (126 shorter events, 21.5 us)
Async XLA Ops:
  0.6 26.5 %copy-start = (f32[1,32]{1,0:T(1,128)S(1)}, f32[1,32]{1,0:T(1,128)}, u32[]{:S(2)}) copy-start(f32[1,32]{1,0:T(1,128)} %param.13) | copy-start | bytes 388
  0.6 17.0 %collective-permute-start = (bf16[1,128,2048]{2,1,0:T(8,128)(2,1)}, bf16[1,128,2048]{2,1,0:T(8,128)(2,1)S(1)}, u32[]{:S(2)}, u32[]{:S(2)}) collective-permute-start(bf16[1,128,2048]{2,1,0:T(8,128)(2,1)} %param.7), channel_id=1, source_target_pairs={{0,64},{64,128},{128,192},{192,256},{256,320},{320,384},{384,448},... | collective-permute-start | bytes 1572872 | tf_op jit(solution)/shard_map/ppermute | solution.py:24
  5.2 1.9 copy-start.11
  5.3 1.9 copy-start.12
  6.7 10.9 %copy-start.7 = (bf16[1,128,2048]{2,1,0:T(8,128)(2,1)S(1)}, bf16[1,128,2048]{2,1,0:T(8,128)(2,1)}, u32[]{:S(2)}) copy-start(bf16[1,128,2048]{2,1,0:T(8,128)(2,1)} %param.7) | copy-start | bytes 1572868
  23.6 34.8 %all-to-all-start = ((bf16[4,1296,128]{2,1,0:T(8,128)(2,1)}), bf16[4,1296,128]{2,1,0:T(8,128)(2,1)S(1)}, u32[]{:S(2)}, u32[]{:S(2)}) async-start(bf16[4,1296,128]{2,1,0:T(8,128)(2,1)} %concatenate.27), calls=%async_computation | async-start | bytes 2654208 | tf_op jit(solution)/shard_map/all_to_all | solution.py:138
  59.4 5.1 %copy-start.20 = (f32[3]{0:T(128)}, f32[3]{0:T(128)S(1)}, u32[]{:S(2)}) copy-start(f32[3]{0:T(128)S(1)} %slice_reduce_fusion.1) | copy-start | bytes 40
  61.5 2.1 copy-start.21
  63.1 1.3 copy-start.16
  64.2 1.2 copy-start.3
  64.4 44.4 %copy-start.15 = (f32[4]{0:T(128)}, f32[4]{0:T(128)S(1)}, u32[]{:S(2)}) copy-start(f32[4]{0:T(128)S(1)} %get-tuple-element.31) | copy-start | bytes 52
  65.4 43.4 %copy-start.1 = (f32[8,128,64]{1,2,0:T(8,128)}, f32[8,128,64]{1,2,0:T(8,128)S(1)}, u32[]{:S(2)}) copy-start(f32[8,128,64]{1,2,0:T(8,128)S(1)} %get-tuple-element.32) | copy-start | bytes 786436
  65.4 12.1 %copy-start.10 = (pred[128,128]{1,0:T(8,128)(4,1)S(1)}, pred[128,128]{1,0:T(8,128)(4,1)}, u32[]{:S(2)}) copy-start(pred[128,128]{1,0:T(8,128)(4,1)} %iota_compare_fusion) | copy-start | bytes 49156
  67.3 42.5 %copy-start.2 = (f32[8,128,64]{1,2,0:T(8,128)}, f32[8,128,64]{1,2,0:T(8,128)S(1)}, u32[]{:S(2)}) copy-start(f32[8,128,64]{1,2,0:T(8,128)S(1)} %get-tuple-element.34) | copy-start | bytes 786436
  67.3 36.8 %copy-start.17 = (f32[8]{0:T(128)S(1)}, f32[8]{0:T(128)}, u32[]{:S(2)}) copy-start(f32[8]{0:T(128)} %copy-done.16) | copy-start | bytes 100
  67.4 18.1 %collective-permute-start.7 = (f32[4,128,64]{1,2,0:T(8,128)S(1)}, f32[4,128,64]{1,2,0:T(8,128)S(1)}, u32[]{:S(2)}, u32[]{:S(2)}) collective-permute-start(f32[4,128,64]{1,2,0:T(8,128)S(1)} %get-tuple-element.25), channel_id=1, source_target_pairs={{16,0},{32,16},{48,32},{17,1},{33,17},{49,33},{18,2},{34,18},{50,3... | collective-permute-start | bytes 393224 | tf_op jit(solution)/shard_map/ppermute | solution.py:24
  68.7 16.8 %collective-permute-start.1 = (f32[4,128,64]{1,2,0:T(8,128)S(1)}, f32[4,128,64]{1,2,0:T(8,128)S(1)}, u32[]{:S(2)}, u32[]{:S(2)}) collective-permute-start(f32[4,128,64]{1,2,0:T(8,128)S(1)} %get-tuple-element.24), channel_id=1, source_target_pairs={{0,16},{16,32},{32,48},{1,17},{17,33},{33,49},{2,18},{18,34},{34,5... | collective-permute-start | bytes 393224 | tf_op jit(solution)/shard_map/ppermute | solution.py:24
  85.6 19.1 %collective-permute-start.8 = (f32[4,128,64]{1,2,0:T(8,128)S(1)}, f32[4,128,64]{1,2,0:T(8,128)S(1)}, u32[]{:S(2)}, u32[]{:S(2)}) collective-permute-start(f32[4,128,64]{1,2,0:T(8,128)S(1)} %get-tuple-element.14), channel_id=1, source_target_pairs={{16,0},{32,16},{48,32},{17,1},{33,17},{49,33},{18,2},{34,18},{50,3... | collective-permute-start | bytes 393224 | tf_op jit(solution)/shard_map/ppermute | solution.py:24
  86.9 21.9 %collective-permute-start.10 = (f32[4,128,64]{1,2,0:T(8,128)S(1)}, f32[4,128,64]{1,2,0:T(8,128)S(1)}, u32[]{:S(2)}, u32[]{:S(2)}) collective-permute-start(f32[4,128,64]{1,2,0:T(8,128)S(1)} %get-tuple-element.15), channel_id=1, source_target_pairs={{16,0},{32,16},{48,32},{17,1},{33,17},{49,33},{18,2},{34,18},{50,3... | collective-permute-start | bytes 393224 | tf_op jit(solution)/shard_map/ppermute | solution.py:24
  88.2 20.6 %collective-permute-start.4 = (f32[4,128,64]{1,2,0:T(8,128)S(1)}, f32[4,128,64]{1,2,0:T(8,128)S(1)}, u32[]{:S(2)}, u32[]{:S(2)}) collective-permute-start(f32[4,128,64]{1,2,0:T(8,128)S(1)} %get-tuple-element.20), channel_id=1, source_target_pairs={{0,16},{16,32},{32,48},{1,17},{17,33},{33,49},{2,18},{18,34},{34,5... | collective-permute-start | bytes 393224 | tf_op jit(solution)/shard_map/ppermute | solution.py:24
  96.8 12.0 %collective-permute-start.2 = (f32[4,128,64]{1,2,0:T(8,128)S(1)}, f32[4,128,64]{1,2,0:T(8,128)S(1)}, u32[]{:S(2)}, u32[]{:S(2)}) collective-permute-start(f32[4,128,64]{1,2,0:T(8,128)S(1)} %get-tuple-element.21), channel_id=1, source_target_pairs={{0,16},{16,32},{32,48},{1,17},{17,33},{33,49},{2,18},{18,34},{34,5... | collective-permute-start | bytes 393224 | tf_op jit(solution)/shard_map/ppermute | solution.py:24
  109.7 15.3 %collective-permute-start.5 = (f32[4,128,64]{1,2,0:T(8,128)}, f32[4,128,64]{1,2,0:T(8,128)}, u32[]{:S(2)}, u32[]{:S(2)}) collective-permute-start(f32[4,128,64]{1,2,0:T(8,128)} %get-tuple-element.22), channel_id=1, source_target_pairs={{0,16},{16,32},{32,48},{1,17},{17,33},{33,49},{2,18},{18,34},{34,5... | collective-permute-start | bytes 393224 | tf_op jit(solution)/shard_map/ppermute | solution.py:24
  118.8 32.7 %collective-permute-start.11 = (f32[4,128,64]{1,2,0:T(8,128)}, f32[4,128,64]{1,2,0:T(8,128)}, u32[]{:S(2)}, u32[]{:S(2)}) collective-permute-start(f32[4,128,64]{1,2,0:T(8,128)} %get-tuple-element.13), channel_id=1, source_target_pairs={{16,0},{32,16},{48,32},{17,1},{33,17},{49,33},{18,2},{34,18},{50,3... | collective-permute-start | bytes 393224 | tf_op jit(solution)/shard_map/ppermute | solution.py:24
  123.1 51.6 %copy-start.13 = (f32[4,8]{0,1:T(8,128)S(1)}, f32[4,8]{0,1:T(8,128)}, u32[]{:S(2)}) copy-start(f32[4,8]{0,1:T(8,128)} %copy.37) | copy-start | bytes 388
  123.8 50.9 %collective-permute-start.9 = (f32[4,128,64]{1,2,0:T(8,128)}, f32[4,128,64]{1,2,0:T(8,128)S(1)}, u32[]{:S(2)}, u32[]{:S(2)}) collective-permute-start(f32[4,128,64]{1,2,0:T(8,128)} %get-tuple-element.12), channel_id=1, source_target_pairs={{16,0},{32,16},{48,32},{17,1},{33,17},{49,33},{18,2},{34,18},{50,3... | collective-permute-start | bytes 393224 | tf_op jit(solution)/shard_map/ppermute | solution.py:24
  153.4 21.3 %collective-permute-start.12 = (f32[4,128,64]{1,2,0:T(8,128)S(1)}, f32[4,128,64]{1,2,0:T(8,128)S(1)}, u32[]{:S(2)}, u32[]{:S(2)}) collective-permute-start(f32[4,128,64]{1,2,0:T(8,128)S(1)} %get-tuple-element.27), channel_id=1, source_target_pairs={{16,0},{32,16},{48,32},{17,1},{33,17},{49,33},{18,2},{34,18},{50,3... | collective-permute-start | bytes 393224 | tf_op jit(solution)/shard_map/ppermute | solution.py:24
  155.3 22.0 %copy-start.18 = (pred[4,4]{0,1:T(4,128)(4,1)}, pred[4,4]{0,1:T(4,128)(4,1)S(1)}, u32[]{:S(2)}) copy-start(pred[4,4]{0,1:T(4,128)(4,1)S(1)} %fusion.61) | copy-start | bytes 52
  155.4 28.7 %collective-permute-start.3 = (f32[4,128,64]{1,2,0:T(8,128)}, f32[4,128,64]{1,2,0:T(8,128)}, u32[]{:S(2)}, u32[]{:S(2)}) collective-permute-start(f32[4,128,64]{1,2,0:T(8,128)} %get-tuple-element.23), channel_id=1, source_target_pairs={{0,16},{16,32},{32,48},{1,17},{17,33},{33,49},{2,18},{18,34},{34,5... | collective-permute-start | bytes 393224 | tf_op jit(solution)/shard_map/ppermute | solution.py:24
  167.4 16.7 %collective-permute-start.6 = (f32[4,128,64]{1,2,0:T(8,128)}, f32[4,128,64]{1,2,0:T(8,128)}, u32[]{:S(2)}, u32[]{:S(2)}) collective-permute-start(f32[4,128,64]{1,2,0:T(8,128)} %get-tuple-element.26), channel_id=1, source_target_pairs={{0,16},{16,32},{32,48},{1,17},{17,33},{33,49},{2,18},{18,34},{34,5... | collective-permute-start | bytes 393224 | tf_op jit(solution)/shard_map/ppermute | solution.py:24
  177.5 1.1 copy-start.8
  182.7 2.3 %copy-start.19 = (pred[4,4]{0,1:T(4,128)(4,1)S(1)}, pred[4,4]{0,1:T(4,128)(4,1)}, u32[]{:S(2)}) copy-start(pred[4,4]{0,1:T(4,128)(4,1)} %copy-done.18) | copy-start | bytes 52
  187.9 1.1 copy-start.9
  (7 other events, 6.7 us)

commit v5 on v3

--- a/solution.py
+++ b/solution.py
@@ -94,6 +94,24 @@
     mixed = mixed + gain_wide * xk.astype(F32)
     grads = grads + gain_wide * gk.astype(F32)
     return mixed, grads
+
+
+def pack(state, gain):
+    heads, rows, width = state.shape
+    corner = (jnp.arange(8)[:, None] == 0) & (jnp.arange(width)[None, :] == 0)
+    tail = gain[:, None, None] * corner[None].astype(F32)
+    return jnp.concatenate([state, tail], axis=1)
+
+
+def scan_four(block, through, steps):
+    rows = block.shape[1]
+    first = from_behind(pack(block, through), "hi", steps)
+    prev_state = first[:, :rows]
+    inclusive = through[:, None, None] * prev_state + block
+    far = through[:, None, None] * prev_state
+    near = from_behind(pack(inclusive, through), "hi", steps)
+    farther = from_behind(far, "hi", 2 * steps)
+    return near[:, :rows] + near[:, rows, 0][:, None, None] * farther
 
 
 def body(emitted, cotangent, b_proj, c_proj, log_decay, starts, skip):
@@ -135,11 +153,15 @@
 
     parts, through, block_end, block_start = local_terms(xk, gk, bk, ck, deck, flk)
 
-    entering_block = jnp.zeros_like(block_end)
-    leaving_block = jnp.zeros_like(block_start)
-    for _ in range(hi_count - 1):
-        entering_block = from_behind(through[:, None, None] * entering_block + block_end, "hi", 1)
-        leaving_block = from_behind(through[:, None, None] * leaving_block + block_start, "hi", -1)
+    if hi_count == 4:
+        entering_block = scan_four(block_end, through, 1)
+        leaving_block = scan_four(block_start, through, -1)
+    else:
+        entering_block = jnp.zeros_like(block_end)
+        leaving_block = jnp.zeros_like(block_start)
+        for _ in range(hi_count - 1):
+            entering_block = from_behind(through[:, None, None] * entering_block + block_end, "hi", 1)
+            leaving_block = from_behind(through[:, None, None] * leaving_block + block_start, "hi", -1)
 
     mixed, grads = finish(parts, xk, gk, bk, ck, gain, entering_block, leaving_block)
     homeward = jnp.concatenate(

time: 214 us -> 293 us (1.37)
  the two profiles are of different devices: /device:TPU:16 before, /device:TPU:32 now
where the time goes in v5:
time: 293 us; the launch traced here: 292 us
  waiting for transfers between devices  98.5 us (34%)
  blocking collectives  71.7 us (24%)
  starting transfers between devices  64.3 us (22%)
  local copies, waits for them, and re-layouts  28.2 us (10%)
  matrix products  16.8 us (6%)
  other arithmetic  11 us (4%)
    all_to_all x1, blocking collectives, body(): lax.all_to_all(homeward, 'lo', split_axis=0, concat_axis=0, tiled=True)  71.7 us
    ppermute x7, waiting for transfers between devices, from_behind(): lax.ppermute(value, axis, [(source, source + steps) for source in range(l...  70.2 us
    ppermute x7, starting transfers between devices, from_behind(): lax.ppermute(value, axis, [(source, source + steps) for source in range(l...  57 us
    all_to_all x1, waiting for transfers between devices, body(): got = lax.all_to_all(payload, 'lo', split_axis=0, concat_axis=0, tiled=True)  28.3 us
    dot_general x4, matrix products, mm_wide(): return jnp.einsum(spec, a.astype(F32), b.astype(F32), precision=HIGH)  9.66 us
    all_to_all x1, starting transfers between devices, body(): got = lax.all_to_all(payload, 'lo', split_axis=0, concat_axis=0, tiled=True)  7.26 us
  transfers between devices with their start and end apart: 8, of which 5 were waited for; matrix products, arithmetic and copies ran while one was open for 9% of the time, Pallas kernels for 0%

profile of v5, /device:TPU:32, one launch (start us, length us, event | category | flops | bytes accessed | tf_op | source)
XLA Modules:
  0.0 292.4 jit_solution(1709929349849531712)
XLA Ops:
  0.6 1.9 collective-permute-start
  2.6 1.4 reshape_squeeze.10
  4.7 7.9 %collective-permute-done = bf16[1,128,2048]{2,1,0:T(8,128)(2,1)S(1)} collective-permute-done((bf16[1,128,2048]{2,1,0:T(8,128)(2,1)}, bf16[1,128,2048]{2,1,0:T(8,128)(2,1)S(1)}, u32[]{:S(2)}, u32[]{:S(2)}) %collective-permute-start) | collective-permute-done | bytes 524320 | tf_op jit(solution)/shard_map/ppermute | solution.py:23
  13.7 4.8 %concatenate.33 = bf16[4,1296,128]{2,1,0:T(8,128)(2,1)} concatenate(bf16[4,512,128]{2,1,0:T(8,128)(2,1)S(1)} %reshape.225, bf16[4,512,128]{2,1,0:T(8,128)(2,1)S(1)} %reshape.226, bf16[4,256,128]{2,1,0:T(8,128)(2,1)S(1)} %broadcast_in_dim.18, bf16[4,8,128]{2,1,0:T(8,128)(2,1)S(1)} %bitcast.136, bf16[4,1,128]{2,1,0:T(2,128)(2,1)S(1)} %broadcast_in_dim.19, ...), dimensions={1} | concatenate | bytes 2654208 | tf_op jit(solution)/shard_map/concatenate | solution.py:139
  18.5 7.3 %all-to-all-start = ((bf16[4,1296,128]{2,1,0:T(8,128)(2,1)}), bf16[4,1296,128]{2,1,0:T(8,128)(2,1)S(1)}, u32[]{:S(2)}, u32[]{:S(2)}) async-start(bf16[4,1296,128]{2,1,0:T(8,128)(2,1)} %concatenate.33), calls=%async_computation | async-start | bytes 2654208 | tf_op jit(solution)/shard_map/all_to_all | solution.py:142
  26.5 28.3 %all-to-all-done = bf16[4,1296,128]{2,1,0:T(8,128)(2,1)S(1)} async-done(((bf16[4,1296,128]{2,1,0:T(8,128)(2,1)}), bf16[4,1296,128]{2,1,0:T(8,128)(2,1)S(1)}, u32[]{:S(2)}, u32[]{:S(2)}) %all-to-all-start) | async-done | bytes 1327136 | tf_op jit(solution)/shard_map/all_to_all | solution.py:142
  60.6 1.4 copy.94
  62.2 2.7 fusion.13
  65.7 11.7 %collective-permute-start.1 = (f32[8,136,64]{1,2,0:T(8,128)}, f32[8,136,64]{1,2,0:T(8,128)}, u32[]{:S(2)}, u32[]{:S(2)}) collective-permute-start(f32[8,136,64]{1,2,0:T(8,128)} %pad_maximum_fusion.4), channel_id=1, source_target_pairs={{0,16},{16,32},{32,48},{1,17},{17,33},{33,49},{2,18},{18,34},{34,5... | collective-permute-start | bytes 835592 | tf_op jit(solution)/shard_map/ppermute | solution.py:23
  77.7 1.6 reshape.229
  79.3 1.4 copy.104
  80.7 1.8 fusion.12
  82.5 5.0 %collective-permute-done.1 = f32[8,136,64]{1,2,0:T(8,128)} collective-permute-done((f32[8,136,64]{1,2,0:T(8,128)}, f32[8,136,64]{1,2,0:T(8,128)}, u32[]{:S(2)}, u32[]{:S(2)}) %collective-permute-start.1) | collective-permute-done | bytes 278560 | tf_op jit(solution)/shard_map/ppermute | solution.py:23
  87.4 1.8 fusion.68
  90.1 1.3 collective-permute-start.4
  94.2 1.3 copy.100
  95.8 24.6 %collective-permute-start.2 = (f32[8,136,64]{1,2,0:T(8,128)S(1)}, f32[8,136,64]{1,2,0:T(8,128)S(1)}, u32[]{:S(2)}, u32[]{:S(2)}) collective-permute-start(f32[8,136,64]{1,2,0:T(8,128)S(1)} %get-tuple-element.18), channel_id=1, source_target_pairs={{0,16},{16,32},{32,48},{1,17},{17,33},{33,49},{2,18},{18,34},{34,5... | collective-permute-start | bytes 835592 | tf_op jit(solution)/shard_map/ppermute | solution.py:23
  120.4 14.8 %collective-permute-start.3 = (f32[8,128,64]{1,2,0:T(8,128)}, f32[8,128,64]{1,2,0:T(8,128)S(1)}, u32[]{:S(2)}, u32[]{:S(2)}) collective-permute-start(f32[8,128,64]{1,2,0:T(8,128)} %get-tuple-element.11), channel_id=1, source_target_pairs={{0,32},{16,48},{1,33},{17,49},{2,34},{18,50},{3,35},{19,51},{4,36}... | collective-permute-start | bytes 786440 | tf_op jit(solution)/shard_map/ppermute | solution.py:23
  135.2 1.8 fusion.69
  137.8 1.3 collective-permute-start.5
  139.1 1.5 collective-permute-start.6
  140.9 2.7 multiply_add_fusion.1
  144.8 3.3 %fusion.9 = bf16[4,128,8,64]{1,3,2,0:T(8,128)(2,1)} fusion(bf16[4,128,8,64]{1,3,2,0:T(8,128)(2,1)S(1)} %copy-done.3, f32[4,128,8,64]{1,3,2,0:T(8,128)S(1)} %bitcast.130, f32[4,128,128]{2,1,0:T(8,128)S(1)} %fusion.33, f32[4,8,128]{2,1,0:T(8,128)S(1)} %fusion.39, pred[4,128,128]{2,1,0:T(8,128)(4,1)S(1)} %compare_and_fusion, f32[8]{0:T(128)S(1)} %copy-done.16, ...), kind=kOutput, calls=%fused_computation.16 | convolution fusion | flops 406323200 | bytes 2457632 | tf_op jit(solution)/shard_map/khtu,kuhp->kthp/dot_general | solution.py:31
  148.1 1.6 copy.103
  149.7 1.3 reshape.228
  151.0 52.0 %collective-permute-done.5 = f32[8,136,64]{1,2,0:T(8,128)} collective-permute-done((f32[8,136,64]{1,2,0:T(8,128)}, f32[8,136,64]{1,2,0:T(8,128)}, u32[]{:S(2)}, u32[]{:S(2)}) %collective-permute-start.5) | collective-permute-done | bytes 278560 | tf_op jit(solution)/shard_map/ppermute | solution.py:23
  203.8 5.4 %collective-permute-done.6 = f32[8,128,64]{1,2,0:T(8,128)} collective-permute-done((f32[8,128,64]{1,2,0:T(8,128)}, f32[8,128,64]{1,2,0:T(8,128)}, u32[]{:S(2)}, u32[]{:S(2)}) %collective-permute-start.6) | collective-permute-done | bytes 262176 | tf_op jit(solution)/shard_map/ppermute | solution.py:23
  209.2 1.1 slice_add_fusion
  210.4 2.7 multiply_add_fusion
  214.3 1.9 fusion.8
  217.3 71.7 %all_to_all.10 = bf16[4,1024,128]{2,1,0:T(8,128)(2,1)S(1)} all-to-all(bf16[4,1024,128]{2,1,0:T(8,128)(2,1)S(1)} %pad_maximum_fusion), channel_id=1, replica_groups=mesh['pipe'=16,'hi'=4,'lo'=4,'tp'=4] {'lo'}, dimensions={0} | all-to-all | bytes 2097152 | tf_op jit(solution)/shard_map/all_to_all | solution.py:170
  289.7 1.0 copy.112
  (107 shorter events, 20.4 us)
Async XLA Ops:
  0.6 25.3 %copy-start = (f32[1,32]{1,0:T(1,128)S(1)}, f32[1,32]{1,0:T(1,128)}, u32[]{:S(2)}) copy-start(f32[1,32]{1,0:T(1,128)} %param.13) | copy-start | bytes 388
  0.6 11.9 %collective-permute-start = (bf16[1,128,2048]{2,1,0:T(8,128)(2,1)}, bf16[1,128,2048]{2,1,0:T(8,128)(2,1)S(1)}, u32[]{:S(2)}, u32[]{:S(2)}) collective-permute-start(bf16[1,128,2048]{2,1,0:T(8,128)(2,1)} %param.7), channel_id=1, source_target_pairs={{0,64},{64,128},{128,192},{192,256},{256,320},{320,384},{384,448},... | collective-permute-start | bytes 1572872 | tf_op jit(solution)/shard_map/ppermute | solution.py:23
  2.6 1.9 copy-start.8
  2.6 1.9 copy-start.9
  4.0 0.7 copy-start.15
  4.1 8.5 %copy-start.5 = (bf16[1,128,2048]{2,1,0:T(8,128)(2,1)S(1)}, bf16[1,128,2048]{2,1,0:T(8,128)(2,1)}, u32[]{:S(2)}) copy-start(bf16[1,128,2048]{2,1,0:T(8,128)(2,1)} %param.7) | copy-start | bytes 1572868
  13.0 0.7 copy-start.11
  18.5 36.3 %all-to-all-start = ((bf16[4,1296,128]{2,1,0:T(8,128)(2,1)}), bf16[4,1296,128]{2,1,0:T(8,128)(2,1)S(1)}, u32[]{:S(2)}, u32[]{:S(2)}) async-start(bf16[4,1296,128]{2,1,0:T(8,128)(2,1)} %concatenate.33), calls=%async_computation | async-start | bytes 2654208 | tf_op jit(solution)/shard_map/all_to_all | solution.py:142
  59.3 28.2 %copy-start.12 = (f32[8]{0:T(128)}, f32[8]{0:T(128)S(1)}, u32[]{:S(2)}) copy-start(f32[8]{0:T(128)S(1)} %exponential_multiply_fusion.2) | copy-start | bytes 100
  65.7 21.7 %collective-permute-start.1 = (f32[8,136,64]{1,2,0:T(8,128)}, f32[8,136,64]{1,2,0:T(8,128)}, u32[]{:S(2)}, u32[]{:S(2)}) collective-permute-start(f32[8,136,64]{1,2,0:T(8,128)} %pad_maximum_fusion.4), channel_id=1, source_target_pairs={{0,16},{16,32},{32,48},{1,17},{17,33},{33,49},{2,18},{18,34},{34,5... | collective-permute-start | bytes 835592 | tf_op jit(solution)/shard_map/ppermute | solution.py:23
  90.1 45.1 %collective-permute-start.4 = (f32[8,136,64]{1,2,0:T(8,128)}, f32[8,136,64]{1,2,0:T(8,128)}, u32[]{:S(2)}, u32[]{:S(2)}) collective-permute-start(f32[8,136,64]{1,2,0:T(8,128)} %get-tuple-element.19), channel_id=1, source_target_pairs={{16,0},{32,16},{48,32},{17,1},{33,17},{49,33},{18,2},{34,18},{50,3... | collective-permute-start | bytes 835592 | tf_op jit(solution)/shard_map/ppermute | solution.py:23
  95.7 48.6 %copy-start.6 = (f32[4,128,128]{2,1,0:T(8,128)}, f32[4,128,128]{2,1,0:T(8,128)S(1)}, u32[]{:S(2)}) copy-start(f32[4,128,128]{2,1,0:T(8,128)S(1)} %fusion.33) | copy-start | bytes 786436
  95.8 44.8 %collective-permute-start.2 = (f32[8,136,64]{1,2,0:T(8,128)S(1)}, f32[8,136,64]{1,2,0:T(8,128)S(1)}, u32[]{:S(2)}, u32[]{:S(2)}) collective-permute-start(f32[8,136,64]{1,2,0:T(8,128)S(1)} %get-tuple-element.18), channel_id=1, source_target_pairs={{0,16},{16,32},{32,48},{1,17},{17,33},{33,49},{2,18},{18,34},{34,5... | collective-permute-start | bytes 835592 | tf_op jit(solution)/shard_map/ppermute | solution.py:23
  120.3 20.5 %copy-start.1 = (f32[4,8,64,128]{3,2,1,0:T(8,128)S(1)}, f32[4,8,64,128]{3,2,1,0:T(8,128)}, u32[]{:S(2)}) copy-start(f32[4,8,64,128]{3,2,1,0:T(8,128)} %get-tuple-element.27) | copy-start | bytes 3145732
  120.4 20.5 %copy-start.10 = (f32[4,8]{0,1:T(8,128)S(1)}, f32[4,8]{0,1:T(8,128)}, u32[]{:S(2)}) copy-start(f32[4,8]{0,1:T(8,128)} %copy.100) | copy-start | bytes 388
  120.4 20.5 %copy-start.13 = (pred[4,4]{0,1:T(4,128)(4,1)S(1)}, pred[4,4]{0,1:T(4,128)(4,1)}, u32[]{:S(2)}) copy-start(pred[4,4]{0,1:T(4,128)(4,1)} %fusion.61) | copy-start | bytes 52
  120.4 20.4 %collective-permute-start.3 = (f32[8,128,64]{1,2,0:T(8,128)}, f32[8,128,64]{1,2,0:T(8,128)S(1)}, u32[]{:S(2)}, u32[]{:S(2)}) collective-permute-start(f32[8,128,64]{1,2,0:T(8,128)} %get-tuple-element.11), channel_id=1, source_target_pairs={{0,32},{16,48},{1,33},{17,49},{2,34},{18,50},{3,35},{19,51},{4,36}... | collective-permute-start | bytes 786440 | tf_op jit(solution)/shard_map/ppermute | solution.py:23
  137.8 65.1 %collective-permute-start.5 = (f32[8,136,64]{1,2,0:T(8,128)}, f32[8,136,64]{1,2,0:T(8,128)}, u32[]{:S(2)}, u32[]{:S(2)}) collective-permute-start(f32[8,136,64]{1,2,0:T(8,128)} %pad_maximum_fusion.1), channel_id=1, source_target_pairs={{16,0},{32,16},{48,32},{17,1},{33,17},{49,33},{18,2},{34,18},{50,3... | collective-permute-start | bytes 835592 | tf_op jit(solution)/shard_map/ppermute | solution.py:23
  139.1 70.1 %collective-permute-start.6 = (f32[8,128,64]{1,2,0:T(8,128)}, f32[8,128,64]{1,2,0:T(8,128)}, u32[]{:S(2)}, u32[]{:S(2)}) collective-permute-start(f32[8,128,64]{1,2,0:T(8,128)} %get-tuple-element.13), channel_id=1, source_target_pairs={{32,0},{48,16},{33,1},{49,17},{34,2},{50,18},{35,3},{51,19},{36,4}... | collective-permute-start | bytes 786440 | tf_op jit(solution)/shard_map/ppermute | solution.py:23
  143.7 1.0 copy-start.3
  143.7 1.0 copy-start.16
  149.7 60.7 %copy-start.14 = (pred[4,4]{0,1:T(4,128)(4,1)S(1)}, pred[4,4]{0,1:T(4,128)(4,1)}, u32[]{:S(2)}) copy-start(pred[4,4]{0,1:T(4,128)(4,1)} %fusion.61) | copy-start | bytes 52
  213.2 1.0 copy-start.2
  213.2 1.1 copy-start.7
  213.2 1.1 copy-start.17
  216.2 1.1 copy-start.4

commit v6 on v3

--- a/solution.py
+++ b/solution.py
@@ -72,7 +72,7 @@
     return parts, through, block_end, block_start
 
 
-def finish(parts, xk, gk, bk, ck, gain, entering_block, leaving_block):
+def finish_local(parts, xk, gk, bk, ck, gain):
     cum, seg, causal = parts["cum"], parts["seg"], parts["causal"]
     linked = (seg[:, :, None] == seg[:, None, :]) & causal[None]
     spread = cum[:, :, :, None] - cum[:, :, None, :]
@@ -85,14 +85,21 @@
     carry = parts["carry"]
     entering = jnp.einsum("kjh,jhnp->khnp", carry, parts["end_states"], precision=HIGH)
     leaving = jnp.einsum("jkh,jhnp->khnp", carry, parts["start_states"], precision=HIGH)
-    entering = entering + parts["from_start"][:, :, None, None] * entering_block[None]
-    leaving = leaving + parts["to_end"][:, :, None, None] * leaving_block[None]
-
     mixed = mixed + parts["inflow_q"] * mm_wide("ktn,khnp->kthp", ck, entering)
     grads = grads + parts["outflow_q"] * mm_wide("kun,khnp->kuhp", bk, leaving)
     gain_wide = gain[None, None, :, None]
     mixed = mixed + gain_wide * xk.astype(F32)
     grads = grads + gain_wide * gk.astype(F32)
+    return mixed, grads
+
+
+def finish_outer(parts, mixed, grads, bk, ck, entering_block, leaving_block):
+    entering_rows = mm_wide("ktn,hnp->kthp", ck, entering_block)
+    leaving_rows = mm_wide("kun,hnp->kuhp", bk, leaving_block)
+    from_start = parts["from_start"][:, None, :, None]
+    to_end = parts["to_end"][:, None, :, None]
+    mixed = mixed + parts["inflow_q"] * (from_start * entering_rows)
+    grads = grads + parts["outflow_q"] * (to_end * leaving_rows)
     return mixed, grads
 
 
@@ -134,6 +141,10 @@
     gain = lax.dynamic_slice_in_dim(skip[0], first_head, head_share)
 
     parts, through, block_end, block_start = local_terms(xk, gk, bk, ck, deck, flk)
+    mixed, grads = finish_local(parts, xk, gk, bk, ck, gain)
+    block_end, block_start, mixed, grads = lax.optimization_barrier(
+        (block_end, block_start, mixed, grads)
+    )
 
     entering_block = jnp.zeros_like(block_end)
     leaving_block = jnp.zeros_like(block_start)
@@ -141,7 +152,7 @@
         entering_block = from_behind(through[:, None, None] * entering_block + block_end, "hi", 1)
         leaving_block = from_behind(through[:, None, None] * leaving_block + block_start, "hi", -1)
 
-    mixed, grads = finish(parts, xk, gk, bk, ck, gain, entering_block, leaving_block)
+    mixed, grads = finish_outer(parts, mixed, grads, bk, ck, entering_block, leaving_block)
     homeward = jnp.concatenate(
         [mixed.reshape(lo_count, rows, 128), grads.reshape(lo_count, rows, 128)], axis=1
     ).astype(BF16)

time: 214 us -> 226 us (1.056)
  the two profiles are of different devices: /device:TPU:16 before, /device:TPU:48 now
where the time goes in v6:
time: 226 us; the launch traced here: 225 us
  waiting for transfers between devices  63 us (28%)
  blocking collectives  58.8 us (26%)
  starting transfers between devices  58.1 us (26%)
  local copies, waits for them, and re-layouts  21.6 us (10%)
  matrix products  18.2 us (8%)
  other arithmetic  3.38 us (1%)
    all_to_all x1, blocking collectives, body(): lax.all_to_all(homeward, 'lo', split_axis=0, concat_axis=0, tiled=True)  58.8 us
    ppermute x7, starting transfers between devices, from_behind(): lax.ppermute(value, axis, [(source, source + steps) for source in range(l...  50.9 us
    ppermute x7, waiting for transfers between devices, from_behind(): lax.ppermute(value, axis, [(source, source + steps) for source in range(l...  33.5 us
    all_to_all x1, waiting for transfers between devices, body(): got = lax.all_to_all(payload, 'lo', split_axis=0, concat_axis=0, tiled=True)  29.6 us
    dot_general x6, matrix products, mm_wide(): return jnp.einsum(spec, a.astype(F32), b.astype(F32), precision=HIGH)  11.4 us
    all_to_all x1, starting transfers between devices, body(): got = lax.all_to_all(payload, 'lo', split_axis=0, concat_axis=0, tiled=True)  7.26 us
    concatenate x1, local copies, waits for them, and re-layouts, body(): jnp.concatenate([to_rows(inputs), to_rows(upstream), proj_rows, decay_row...  4.78 us
  transfers between devices with their start and end apart: 8, of which 6 were waited for; matrix products, arithmetic and copies ran while one was open for 2% of the time, Pallas kernels for 0%

profile of v6, /device:TPU:48, one launch (start us, length us, event | category | flops | bytes accessed | tf_op | source)
XLA Modules:
  0.0 224.9 jit_solution(14122978656249767607)
XLA Ops:
  0.6 1.9 collective-permute-start
  2.6 1.4 reshape_squeeze.10
  4.7 6.6 %collective-permute-done = bf16[1,128,2048]{2,1,0:T(8,128)(2,1)S(1)} collective-permute-done((bf16[1,128,2048]{2,1,0:T(8,128)(2,1)}, bf16[1,128,2048]{2,1,0:T(8,128)(2,1)S(1)}, u32[]{:S(2)}, u32[]{:S(2)}) %collective-permute-start) | collective-permute-done | bytes 524320 | tf_op jit(solution)/shard_map/ppermute | solution.py:23
  12.5 4.8 %concatenate.23 = bf16[4,1296,128]{2,1,0:T(8,128)(2,1)} concatenate(bf16[4,512,128]{2,1,0:T(8,128)(2,1)S(1)} %reshape.185, bf16[4,512,128]{2,1,0:T(8,128)(2,1)S(1)} %reshape.186, bf16[4,256,128]{2,1,0:T(8,128)(2,1)S(1)} %broadcast_in_dim.18, bf16[4,8,128]{2,1,0:T(8,128)(2,1)S(1)} %bitcast.135, bf16[4,1,128]{2,1,0:T(2,128)(2,1)S(1)} %broadcast_in_dim.19, ...), dimensions={1} | concatenate | bytes 2654208 | tf_op jit(solution)/shard_map/concatenate | solution.py:128
  17.3 7.3 %all-to-all-start = ((bf16[4,1296,128]{2,1,0:T(8,128)(2,1)}), bf16[4,1296,128]{2,1,0:T(8,128)(2,1)S(1)}, u32[]{:S(2)}, u32[]{:S(2)}) async-start(bf16[4,1296,128]{2,1,0:T(8,128)(2,1)} %concatenate.23), calls=%async_computation | async-start | bytes 2654208 | tf_op jit(solution)/shard_map/all_to_all | solution.py:131
  24.5 0.7 dynamic-slice_bitcast_fusion
  25.2 29.6 %all-to-all-done = bf16[4,1296,128]{2,1,0:T(8,128)(2,1)S(1)} async-done(((bf16[4,1296,128]{2,1,0:T(8,128)(2,1)}), bf16[4,1296,128]{2,1,0:T(8,128)(2,1)S(1)}, u32[]{:S(2)}, u32[]{:S(2)}) %all-to-all-start) | async-done | bytes 1327136 | tf_op jit(solution)/shard_map/all_to_all | solution.py:131
  57.3 0.9 fusion.70
  60.0 1.1 compare_convert_fusion.3
  61.4 1.4 fusion.16
  62.7 2.5 %convolution_bitcast_fusion = f32[4,8,128,64]{2,0,3,1:T(4,128)S(1)} fusion(f32[4,8,128,64]{2,3,1,0:T(8,128)S(1)} %bitcast.119, f32[4,8]{0,1:T(8,128)S(1)} %copy.29, f32[4,8]{0,1:T(8,128)S(1)} %concatenate.24.clone, pred[4,4]{0,1:T(4,128)(4,1)S(1)} %fusion.63), kind=kOutput, calls=%fused_computation.5 | convolution fusion | flops 12583296 | bytes 2097424 | tf_op jit(solution)/shard_map/jkh,jhnp->khnp/dot_general | solution.py:87
  65.5 1.6 reshape.188
  67.2 1.4 copy.25
  68.6 0.7 fusion.77
  69.3 2.4 %fusion.17 = (f32[8,128,64]{1,2,0:T(8,128)}, f32[4,8,64,128]{3,2,1,0:T(8,128)S(1)}) fusion(f32[8,4]{0,1:T(4,128)S(1)} %fusion.77, bf16[4,1296,128]{2,1,0:T(8,128)(2,1)S(1)} %all-to-all-done, bf16[4,128,8,64]{1,3,2,0:T(8,128)(2,1)} %copy.25, f32[4,128,8]{1,2,0:T(8,128)S(1)} %get-tuple-element.19), kind=kOutput, calls=%fused_computation.29 | convolution fusion | flops 403636224 | bytes 1984512 | tf_op jit(solution)/shard_map/kun,kuhp->khnp/dot_general | solution.py:31
  71.7 2.6 %convolution_bitcast_fusion.1 = f32[4,8,128,64]{2,0,3,1:T(4,128)S(1)} fusion(f32[4,8,128,64]{2,3,1,0:T(8,128)S(1)} %bitcast.118, f32[4,8]{0,1:T(8,128)S(1)} %copy.29, f32[4,8]{0,1:T(8,128)S(1)} %concatenate.24.clone, pred[4,4]{0,1:T(4,128)(4,1)S(1)} %copy-done.11), kind=kOutput, calls=%fused_computation.6 | convolution fusion | flops 12583296 | bytes 2097424 | tf_op jit(solution)/shard_map/kjh,jhnp->khnp/dot_general | solution.py:86
  75.5 2.6 %fusion.11 = f32[4,128,8,64]{1,3,2,0:T(8,128)} fusion(bf16[4,128,8,64]{1,3,2,0:T(8,128)(2,1)S(1)} %copy-done.4, f32[4,128,8,64]{1,3,2,0:T(8,128)S(1)} %bitcast.129, f32[4,128,128]{2,1,0:T(8,128)S(1)} %fusion.41, f32[4,8,128]{2,1,0:T(8,128)S(1)} %fusion.49, pred[4,128,128]{2,1,0:T(8,128)(4,1)S(1)} %compare_and_fusion, f32[8]{0:T(128)S(1)} %copy-done.17, ...), kind=kOutput, calls=%fused_computation.20 | convolution fusion | flops 406061056 | bytes 2981920 | tf_op jit(solution)/shard_map/khtu,kthp->kuhp/dot_general | solution.py:31
  79.1 2.4 %fusion.10 = f32[4,128,8,64]{1,3,2,0:T(8,128)S(1)} fusion(bf16[4,128,8,64]{1,3,2,0:T(8,128)(2,1)S(1)} %copy-done.5, f32[4,128,8,64]{1,3,2,0:T(8,128)S(1)} %bitcast.128, f32[4,128,128]{2,1,0:T(8,128)S(1)} %fusion.41, f32[4,8,128]{2,1,0:T(8,128)S(1)} %fusion.49, pred[4,128,128]{2,1,0:T(8,128)(4,1)S(1)} %compare_and_fusion, f32[8]{0:T(128)S(1)} %copy-done.17, ...), kind=kOutput, calls=%fused_computation.19 | convolution fusion | flops 406061056 | bytes 2981920 | tf_op jit(solution)/shard_map/khtu,kuhp->kthp/dot_general | solution.py:31
  81.8 10.9 %collective-permute-start.1 = (f32[8,128,64]{1,2,0:T(8,128)S(1)}, f32[8,128,64]{1,2,0:T(8,128)S(1)}, u32[]{:S(2)}, u32[]{:S(2)}) collective-permute-start(f32[8,128,64]{1,2,0:T(8,128)S(1)} %get-tuple-element.24), channel_id=1, source_target_pairs={{0,16},{16,32},{32,48},{1,17},{17,33},{33,49},{2,18},{18,34},{34,5... | collective-permute-start | bytes 786440 | tf_op jit(solution)/shard_map/ppermute | solution.py:23
  92.7 1.3 collective-permute-start.4
  94.0 3.6 %collective-permute-done.1 = f32[8,128,64]{1,2,0:T(8,128)S(1)} collective-permute-done((f32[8,128,64]{1,2,0:T(8,128)S(1)}, f32[8,128,64]{1,2,0:T(8,128)S(1)}, u32[]{:S(2)}, u32[]{:S(2)}) %collective-permute-start.1) | collective-permute-done | bytes 262176 | tf_op jit(solution)/shard_map/ppermute | solution.py:23
  97.7 15.0 %collective-permute-start.2 = (f32[8,128,64]{1,2,0:T(8,128)S(1)}, f32[8,128,64]{1,2,0:T(8,128)S(1)}, u32[]{:S(2)}, u32[]{:S(2)}) collective-permute-start(f32[8,128,64]{1,2,0:T(8,128)S(1)} %multiply_add_fusion.3), channel_id=1, source_target_pairs={{0,16},{16,32},{32,48},{1,17},{17,33},{33,49},{2,18},{18,34},{34,5... | collective-permute-start | bytes 786440 | tf_op jit(solution)/shard_map/ppermute | solution.py:23
  112.7 6.7 %collective-permute-done.4 = f32[8,128,64]{1,2,0:T(8,128)S(1)} collective-permute-done((f32[8,128,64]{1,2,0:T(8,128)S(1)}, f32[8,128,64]{1,2,0:T(8,128)S(1)}, u32[]{:S(2)}, u32[]{:S(2)}) %collective-permute-start.4) | collective-permute-done | bytes 262176 | tf_op jit(solution)/shard_map/ppermute | solution.py:23
  119.5 1.3 collective-permute-start.5
  120.9 19.1 %collective-permute-start.3 = (f32[8,128,64]{1,2,0:T(8,128)S(1)}, f32[8,128,64]{1,2,0:T(8,128)S(1)}, u32[]{:S(2)}, u32[]{:S(2)}) collective-permute-start(f32[8,128,64]{1,2,0:T(8,128)S(1)} %get-tuple-element.22), channel_id=1, source_target_pairs={{0,16},{16,32},{32,48},{1,17},{17,33},{33,49},{2,18},{18,34},{34,5... | collective-permute-start | bytes 786440 | tf_op jit(solution)/shard_map/ppermute | solution.py:23
  140.1 3.3 %collective-permute-done.5 = f32[8,128,64]{1,2,0:T(8,128)S(1)} collective-permute-done((f32[8,128,64]{1,2,0:T(8,128)S(1)}, f32[8,128,64]{1,2,0:T(8,128)S(1)}, u32[]{:S(2)}, u32[]{:S(2)}) %collective-permute-start.5) | collective-permute-done | bytes 262176 | tf_op jit(solution)/shard_map/ppermute | solution.py:23
  143.5 1.3 collective-permute-start.6
  146.5 13.2 %collective-permute-done.6 = f32[8,128,64]{1,2,0:T(8,128)S(1)} collective-permute-done((f32[8,128,64]{1,2,0:T(8,128)S(1)}, f32[8,128,64]{1,2,0:T(8,128)S(1)}, u32[]{:S(2)}, u32[]{:S(2)}) %collective-permute-start.6) | collective-permute-done | bytes 262176 | tf_op jit(solution)/shard_map/ppermute | solution.py:23
  159.8 1.9 fusion.13
  162.8 58.8 %all_to_all.10 = bf16[4,1024,128]{2,1,0:T(8,128)(2,1)S(1)} all-to-all(bf16[4,1024,128]{2,1,0:T(8,128)(2,1)S(1)} %pad_maximum_fusion), channel_id=1, replica_groups=mesh['pipe'=16,'hi'=4,'lo'=4,'tp'=4] {'lo'}, dimensions={0} | all-to-all | bytes 2097152 | tf_op jit(solution)/shard_map/all_to_all | solution.py:159
  222.3 1.0 copy.40
  223.9 1.0 copy.41
  (97 shorter events, 12.6 us)
Async XLA Ops:
  0.6 23.9 %copy-start = (f32[1,32]{1,0:T(1,128)S(1)}, f32[1,32]{1,0:T(1,128)}, u32[]{:S(2)}) copy-start(f32[1,32]{1,0:T(1,128)} %param.13) | copy-start | bytes 388
  0.6 10.7 %collective-permute-start = (bf16[1,128,2048]{2,1,0:T(8,128)(2,1)}, bf16[1,128,2048]{2,1,0:T(8,128)(2,1)S(1)}, u32[]{:S(2)}, u32[]{:S(2)}) collective-permute-start(bf16[1,128,2048]{2,1,0:T(8,128)(2,1)} %param.7), channel_id=1, source_target_pairs={{0,64},{64,128},{128,192},{192,256},{256,320},{320,384},{384,448},... | collective-permute-start | bytes 1572872 | tf_op jit(solution)/shard_map/ppermute | solution.py:23
  2.6 1.9 copy-start.7
  2.6 1.9 copy-start.8
  4.0 0.7 copy-start.16
  4.1 7.3 %copy-start.6 = (bf16[1,128,2048]{2,1,0:T(8,128)(2,1)S(1)}, bf16[1,128,2048]{2,1,0:T(8,128)(2,1)}, u32[]{:S(2)}) copy-start(bf16[1,128,2048]{2,1,0:T(8,128)(2,1)} %param.7) | copy-start | bytes 1572868
  11.8 0.7 copy-start.9
  17.3 37.5 %all-to-all-start = ((bf16[4,1296,128]{2,1,0:T(8,128)(2,1)}), bf16[4,1296,128]{2,1,0:T(8,128)(2,1)S(1)}, u32[]{:S(2)}, u32[]{:S(2)}) async-start(bf16[4,1296,128]{2,1,0:T(8,128)(2,1)} %concatenate.23), calls=%async_computation | async-start | bytes 2654208 | tf_op jit(solution)/shard_map/all_to_all | solution.py:131
  55.5 3.1 %copy-start.12 = (f32[4]{0:T(128)}, f32[4]{0:T(128)S(1)}, u32[]{:S(2)}) copy-start(f32[4]{0:T(128)S(1)} %compare_convert_fusion.1) | copy-start | bytes 52
  59.2 3.5 %copy-start.3 = (bf16[4,128,8,64]{1,3,2,0:T(8,128)(2,1)}, bf16[4,128,8,64]{1,3,2,0:T(8,128)(2,1)S(1)}, u32[]{:S(2)}) copy-start(bf16[4,128,8,64]{1,3,2,0:T(8,128)(2,1)S(1)} %copy.26) | copy-start | bytes 1572868
  61.2 4.0 %copy-start.10 = (pred[4,4]{0,1:T(4,128)(4,1)}, pred[4,4]{0,1:T(4,128)(4,1)S(1)}, u32[]{:S(2)}) copy-start(pred[4,4]{0,1:T(4,128)(4,1)S(1)} %fusion.63) | copy-start | bytes 52
  68.6 3.1 %copy-start.11 = (pred[4,4]{0,1:T(4,128)(4,1)S(1)}, pred[4,4]{0,1:T(4,128)(4,1)}, u32[]{:S(2)}) copy-start(pred[4,4]{0,1:T(4,128)(4,1)} %copy-done.10) | copy-start | bytes 52
  74.4 1.0 copy-start.4
  74.4 1.0 copy-start.17
  78.1 1.0 copy-start.5
  79.1 2.5 %copy-start.1 = (f32[8,128,64]{1,2,0:T(8,128)S(1)}, f32[8,128,64]{1,2,0:T(8,128)}, u32[]{:S(2)}) copy-start(f32[8,128,64]{1,2,0:T(8,128)} %get-tuple-element.9) | copy-start | bytes 786436
  79.1 2.5 %copy-start.2 = (f32[8,128,64]{1,2,0:T(8,128)S(1)}, f32[8,128,64]{1,2,0:T(8,128)}, u32[]{:S(2)}) copy-start(f32[8,128,64]{1,2,0:T(8,128)} %get-tuple-element.7) | copy-start | bytes 786436
  81.7 39.1 %copy-start.14 = (f32[8]{0:T(128)S(1)}, f32[8]{0:T(128)}, u32[]{:S(2)}) copy-start(f32[8]{0:T(128)} %slice_bitcast_fusion) | copy-start | bytes 100
  81.7 39.1 %copy-start.15 = (f32[4]{0:T(128)S(1)}, f32[4]{0:T(128)}, u32[]{:S(2)}) copy-start(f32[4]{0:T(128)} %compare_convert_fusion.3) | copy-start | bytes 52
  81.8 58.3 %copy-start.13 = (f32[4]{0:T(128)S(1)}, f32[4]{0:T(128)}, u32[]{:S(2)}) copy-start(f32[4]{0:T(128)} %copy-done.12) | copy-start | bytes 52
  81.8 15.8 %collective-permute-start.1 = (f32[8,128,64]{1,2,0:T(8,128)S(1)}, f32[8,128,64]{1,2,0:T(8,128)S(1)}, u32[]{:S(2)}, u32[]{:S(2)}) collective-permute-start(f32[8,128,64]{1,2,0:T(8,128)S(1)} %get-tuple-element.24), channel_id=1, source_target_pairs={{0,16},{16,32},{32,48},{1,17},{17,33},{33,49},{2,18},{18,34},{34,5... | collective-permute-start | bytes 786440 | tf_op jit(solution)/shard_map/ppermute | solution.py:23
  92.7 26.7 %collective-permute-start.4 = (f32[8,128,64]{1,2,0:T(8,128)S(1)}, f32[8,128,64]{1,2,0:T(8,128)S(1)}, u32[]{:S(2)}, u32[]{:S(2)}) collective-permute-start(f32[8,128,64]{1,2,0:T(8,128)S(1)} %get-tuple-element.25), channel_id=1, source_target_pairs={{16,0},{32,16},{48,32},{17,1},{33,17},{49,33},{18,2},{34,18},{50,3... | collective-permute-start | bytes 786440 | tf_op jit(solution)/shard_map/ppermute | solution.py:23
  97.7 21.7 %collective-permute-start.2 = (f32[8,128,64]{1,2,0:T(8,128)S(1)}, f32[8,128,64]{1,2,0:T(8,128)S(1)}, u32[]{:S(2)}, u32[]{:S(2)}) collective-permute-start(f32[8,128,64]{1,2,0:T(8,128)S(1)} %multiply_add_fusion.3), channel_id=1, source_target_pairs={{0,16},{16,32},{32,48},{1,17},{17,33},{33,49},{2,18},{18,34},{34,5... | collective-permute-start | bytes 786440 | tf_op jit(solution)/shard_map/ppermute | solution.py:23
  119.5 23.9 %collective-permute-start.5 = (f32[8,128,64]{1,2,0:T(8,128)S(1)}, f32[8,128,64]{1,2,0:T(8,128)S(1)}, u32[]{:S(2)}, u32[]{:S(2)}) collective-permute-start(f32[8,128,64]{1,2,0:T(8,128)S(1)} %get-tuple-element.23), channel_id=1, source_target_pairs={{16,0},{32,16},{48,32},{17,1},{33,17},{49,33},{18,2},{34,18},{50,3... | collective-permute-start | bytes 786440 | tf_op jit(solution)/shard_map/ppermute | solution.py:23
  120.9 23.9 %collective-permute-start.3 = (f32[8,128,64]{1,2,0:T(8,128)S(1)}, f32[8,128,64]{1,2,0:T(8,128)S(1)}, u32[]{:S(2)}, u32[]{:S(2)}) collective-permute-start(f32[8,128,64]{1,2,0:T(8,128)S(1)} %get-tuple-element.22), channel_id=1, source_target_pairs={{0,16},{16,32},{32,48},{1,17},{17,33},{33,49},{2,18},{18,34},{34,5... | collective-permute-start | bytes 786440 | tf_op jit(solution)/shard_map/ppermute | solution.py:23
  143.5 16.3 %collective-permute-start.6 = (f32[8,128,64]{1,2,0:T(8,128)S(1)}, f32[8,128,64]{1,2,0:T(8,128)S(1)}, u32[]{:S(2)}, u32[]{:S(2)}) collective-permute-start(f32[8,128,64]{1,2,0:T(8,128)S(1)} %multiply_add_fusion), channel_id=1, source_target_pairs={{16,0},{32,16},{48,32},{17,1},{33,17},{49,33},{18,2},{34,18},{50,3... | collective-permute-start | bytes 786440 | tf_op jit(solution)/shard_map/ppermute | solution.py:23

commit v7 on v3

--- a/solution.py
+++ b/solution.py
@@ -21,6 +21,11 @@
     count = lax.axis_size(axis)
     leading, last = (max(0, -steps), min(count, count - steps))
     return lax.ppermute(value, axis, [(source, source + steps) for source in range(leading, last)])
+
+
+def ring_shift(value, axis, steps):
+    count = lax.axis_size(axis)
+    return lax.ppermute(value, axis, [(source, (source + steps) % count) for source in range(count)])
 
 
 def mm(spec, a, b):
@@ -137,9 +142,16 @@
 
     entering_block = jnp.zeros_like(block_end)
     leaving_block = jnp.zeros_like(block_start)
+    hi_pos = lax.axis_index("hi")
     for _ in range(hi_count - 1):
-        entering_block = from_behind(through[:, None, None] * entering_block + block_end, "hi", 1)
-        leaving_block = from_behind(through[:, None, None] * leaving_block + block_start, "hi", -1)
+        entering_block = jnp.where(
+            hi_pos == 0, 0.0, ring_shift(through[:, None, None] * entering_block + block_end, "hi", 1)
+        )
+        leaving_block = jnp.where(
+            hi_pos == hi_count - 1,
+            0.0,
+            ring_shift(through[:, None, None] * leaving_block + block_start, "hi", -1),
+        )
 
     mixed, grads = finish(parts, xk, gk, bk, ck, gain, entering_block, leaving_block)
     homeward = jnp.concatenate(

time: 214 us -> 218 us (1.019)
  the two profiles are of different devices: /device:TPU:16 before, /device:TPU:26 now
where the time goes in v7:
time: 218 us; the launch traced here: 217 us
  waiting for transfers between devices  72.4 us (33%)
  starting transfers between devices  66.3 us (30%)
  blocking collectives  27.5 us (13%)
  local copies, waits for them, and re-layouts  26.5 us (12%)
  matrix products  16.1 us (7%)
  other arithmetic  6.62 us (3%)
    ppermute x6, starting transfers between devices, ring_shift(): lax.ppermute(value, axis, [(source, (source + steps) % count) for source...  57.1 us
    ppermute x6, waiting for transfers between devices, ring_shift(): lax.ppermute(value, axis, [(source, (source + steps) % count) for source...  34.1 us
    all_to_all x1, waiting for transfers between devices, body(): got = lax.all_to_all(payload, 'lo', split_axis=0, concat_axis=0, tiled=True)  31.7 us
    all_to_all x1, blocking collectives, body(): lax.all_to_all(homeward, 'lo', split_axis=0, concat_axis=0, tiled=True)  27.5 us
    dot_general x4, matrix products, mm_wide(): return jnp.einsum(spec, a.astype(F32), b.astype(F32), precision=HIGH)  7.55 us
    all_to_all x1, starting transfers between devices, body(): got = lax.all_to_all(payload, 'lo', split_axis=0, concat_axis=0, tiled=True)  7.26 us
    ppermute x1, waiting for transfers between devices, from_behind(): lax.ppermute(value, axis, [(source, source + steps) for source in range(l...  6.65 us
    concatenate x1, local copies, waits for them, and re-layouts, body(): jnp.concatenate([to_rows(inputs), to_rows(upstream), proj_rows, decay_row...  4.78 us
  transfers between devices with their start and end apart: 8, of which 5 were waited for; matrix products, arithmetic and copies ran while one was open for 10% of the time, Pallas kernels for 0%

profile of v7, /device:TPU:26, one launch (start us, length us, event | category | flops | bytes accessed | tf_op | source)
XLA Modules:
  0.0 217.3 jit_solution(18126378404790323694)
XLA Ops:
  0.6 1.9 collective-permute-start
  2.6 1.4 reshape_squeeze.10
  4.7 6.6 %collective-permute-done = bf16[1,128,2048]{2,1,0:T(8,128)(2,1)S(1)} collective-permute-done((bf16[1,128,2048]{2,1,0:T(8,128)(2,1)}, bf16[1,128,2048]{2,1,0:T(8,128)(2,1)S(1)}, u32[]{:S(2)}, u32[]{:S(2)}) %collective-permute-start) | collective-permute-done | bytes 524320 | tf_op jit(solution)/shard_map/ppermute | solution.py:23
  12.5 4.8 %concatenate.21 = bf16[4,1296,128]{2,1,0:T(8,128)(2,1)} concatenate(bf16[4,512,128]{2,1,0:T(8,128)(2,1)S(1)} %reshape.186, bf16[4,512,128]{2,1,0:T(8,128)(2,1)S(1)} %reshape.187, bf16[4,256,128]{2,1,0:T(8,128)(2,1)S(1)} %broadcast_in_dim.32, bf16[4,8,128]{2,1,0:T(8,128)(2,1)S(1)} %bitcast.137, bf16[4,1,128]{2,1,0:T(2,128)(2,1)S(1)} %broadcast_in_dim.33, ...), dimensions={1} | concatenate | bytes 2654208 | tf_op jit(solution)/shard_map/concatenate | solution.py:126
  17.3 7.3 %all-to-all-start = ((bf16[4,1296,128]{2,1,0:T(8,128)(2,1)}), bf16[4,1296,128]{2,1,0:T(8,128)(2,1)S(1)}, u32[]{:S(2)}, u32[]{:S(2)}) async-start(bf16[4,1296,128]{2,1,0:T(8,128)(2,1)} %concatenate.21), calls=%async_computation | async-start | bytes 2654208 | tf_op jit(solution)/shard_map/all_to_all | solution.py:129
  25.2 31.7 %all-to-all-done = bf16[4,1296,128]{2,1,0:T(8,128)(2,1)S(1)} async-done(((bf16[4,1296,128]{2,1,0:T(8,128)(2,1)}), bf16[4,1296,128]{2,1,0:T(8,128)(2,1)S(1)}, u32[]{:S(2)}, u32[]{:S(2)}) %all-to-all-start) | async-done | bytes 1327136 | tf_op jit(solution)/shard_map/all_to_all | solution.py:129
  58.0 0.9 fusion.68
  61.8 1.6 reshape.188
  63.5 1.4 copy.25
  65.9 1.7 fusion.13
  67.7 10.9 %collective-permute-start.1 = (f32[8,128,64]{1,2,0:T(8,128)S(1)}, f32[8,128,64]{1,2,0:T(8,128)S(1)}, u32[]{:S(2)}, u32[]{:S(2)}) collective-permute-start(f32[8,128,64]{1,2,0:T(8,128)S(1)} %get-tuple-element.16), channel_id=1, source_target_pairs={{0,16},{16,32},{32,48},{48,0},{1,17},{17,33},{33,49},{49,1},{2,18}... | collective-permute-start | bytes 786440 | tf_op jit(solution)/shard_map/ppermute | solution.py:28
  79.3 6.5 %collective-permute-start.4 = (f32[8,128,64]{1,2,0:T(8,128)S(1)}, f32[8,128,64]{1,2,0:T(8,128)S(1)}, u32[]{:S(2)}, u32[]{:S(2)}) collective-permute-start(f32[8,128,64]{1,2,0:T(8,128)S(1)} %get-tuple-element.17), channel_id=1, source_target_pairs={{0,48},{16,0},{32,16},{48,32},{1,49},{17,1},{33,17},{49,33},{2,50}... | collective-permute-start | bytes 786440 | tf_op jit(solution)/shard_map/ppermute | solution.py:28
  85.9 10.3 %collective-permute-done.1 = f32[8,128,64]{1,2,0:T(8,128)S(1)} collective-permute-done((f32[8,128,64]{1,2,0:T(8,128)S(1)}, f32[8,128,64]{1,2,0:T(8,128)S(1)}, u32[]{:S(2)}, u32[]{:S(2)}) %collective-permute-start.1) | collective-permute-done | bytes 262176 | tf_op jit(solution)/shard_map/ppermute | solution.py:28
  96.3 12.9 %collective-permute-start.2 = (f32[8,128,64]{1,2,0:T(8,128)S(1)}, f32[8,128,64]{1,2,0:T(8,128)S(1)}, u32[]{:S(2)}, u32[]{:S(2)}) collective-permute-start(f32[8,128,64]{1,2,0:T(8,128)S(1)} %multiply_add_fusion.5), channel_id=1, source_target_pairs={{0,16},{16,32},{32,48},{48,0},{1,17},{17,33},{33,49},{49,1},{2,18}... | collective-permute-start | bytes 786440 | tf_op jit(solution)/shard_map/ppermute | solution.py:28
  109.8 0.9 fusion.33
  110.8 21.2 %collective-permute-done.2 = f32[8,128,64]{1,2,0:T(8,128)S(1)} collective-permute-done((f32[8,128,64]{1,2,0:T(8,128)S(1)}, f32[8,128,64]{1,2,0:T(8,128)S(1)}, u32[]{:S(2)}, u32[]{:S(2)}) %collective-permute-start.2) | collective-permute-done | bytes 262176 | tf_op jit(solution)/shard_map/ppermute | solution.py:28
  132.1 19.5 %collective-permute-start.5 = (f32[8,128,64]{1,2,0:T(8,128)S(1)}, f32[8,128,64]{1,2,0:T(8,128)}, u32[]{:S(2)}, u32[]{:S(2)}) collective-permute-start(f32[8,128,64]{1,2,0:T(8,128)S(1)} %get-tuple-element.15), channel_id=1, source_target_pairs={{0,48},{16,0},{32,16},{48,32},{1,49},{17,1},{33,17},{49,33},{2,50}... | collective-permute-start | bytes 786440 | tf_op jit(solution)/shard_map/ppermute | solution.py:28
  151.7 1.9 collective-permute-start.3
  156.5 1.3 copy.31
  157.8 2.5 %collective-permute-done.5 = f32[8,128,64]{1,2,0:T(8,128)} collective-permute-done((f32[8,128,64]{1,2,0:T(8,128)S(1)}, f32[8,128,64]{1,2,0:T(8,128)}, u32[]{:S(2)}, u32[]{:S(2)}) %collective-permute-start.5) | collective-permute-done | bytes 262176 | tf_op jit(solution)/shard_map/ppermute | solution.py:28
  160.4 1.8 multiply_add_fusion.2
  162.1 5.4 %collective-permute-start.6 = (f32[8,128,64]{1,2,0:T(8,128)}, f32[8,128,64]{1,2,0:T(8,128)}, u32[]{:S(2)}, u32[]{:S(2)}) collective-permute-start(f32[8,128,64]{1,2,0:T(8,128)} %multiply_add_fusion.2), channel_id=1, source_target_pairs={{0,48},{16,0},{32,16},{48,32},{1,49},{17,1},{33,17},{49,33},{2,50}... | collective-permute-start | bytes 786440 | tf_op jit(solution)/shard_map/ppermute | solution.py:28
  167.6 3.4 %multiply_add_fusion.1 = f32[4,8,128,64]{2,0,3,1:T(4,128)S(1)} fusion(f32[8,128,64]{1,2,0:T(8,128)S(1)} %broadcast_select_fusion.2, f32[4,8]{0,1:T(8,128)} %copy.31, f32[4,8,128,64]{2,3,1,0:T(8,128)S(1)} %bitcast.123, f32[4,8]{0,1:T(8,128)S(1)} %copy.28, f32[4,8]{0,1:T(8,128)S(1)} %concatenate.23.clone, pred[4,4]{0,1:T(4,128)(4,1)} %fusion.61), kind=kOutput, calls=%fused_computation.27 | convolution fusion | flops 13107584 | bytes 2359696 | tf_op jit(solution)/shard_map/kjh,jhnp->khnp/dot_general | solution.py:91
  172.3 3.3 %fusion.9 = bf16[4,128,8,64]{1,3,2,0:T(8,128)(2,1)} fusion(bf16[4,128,8,64]{1,3,2,0:T(8,128)(2,1)S(1)} %copy-done.5, f32[4,128,8,64]{1,3,2,0:T(8,128)S(1)} %bitcast.131, f32[4,128,128]{2,1,0:T(8,128)S(1)} %copy-done.8, f32[4,8,128]{2,1,0:T(8,128)S(1)} %fusion.39, pred[4,128,128]{2,1,0:T(8,128)(4,1)S(1)} %compare_and_fusion, f32[8]{0:T(128)S(1)} %copy-done.16, ...), kind=kOutput, calls=%fused_computation.16 | convolution fusion | flops 406323200 | bytes 2457632 | tf_op jit(solution)/shard_map/khtu,kuhp->kthp/dot_general | solution.py:36
  175.6 1.6 copy.33
  177.2 1.3 reshape.189
  178.5 1.0 broadcast_select_fusion.1
  179.4 2.7 %multiply_add_fusion = f32[4,8,128,64]{2,0,3,1:T(4,128)S(1)} fusion(f32[8,128,64]{1,2,0:T(8,128)S(1)} %broadcast_select_fusion.1, f32[4,8]{0,1:T(8,128)S(1)} %copy.37, f32[4,8,128,64]{2,3,1,0:T(8,128)S(1)} %bitcast.122, f32[4,8]{0,1:T(8,128)S(1)} %copy.28, f32[4,8]{0,1:T(8,128)S(1)} %concatenate.23.clone, pred[4,4]{0,1:T(4,128)(4,1)S(1)} %copy-done.14), kind=kOutput, calls=%fused_computation.26 | convolution fusion | flops 13107584 | bytes 2359696 | tf_op jit(solution)/shard_map/jkh,jhnp->khnp/dot_general | solution.py:92
  183.4 1.9 fusion.8
  186.4 27.5 %all_to_all.10 = bf16[4,1024,128]{2,1,0:T(8,128)(2,1)S(1)} all-to-all(bf16[4,1024,128]{2,1,0:T(8,128)(2,1)S(1)} %pad_maximum_fusion), channel_id=1, replica_groups=mesh['pipe'=16,'hi'=4,'lo'=4,'tp'=4] {'lo'}, dimensions={0} | all-to-all | bytes 2097152 | tf_op jit(solution)/shard_map/all_to_all | solution.py:160
  214.6 1.0 copy.42
  216.2 1.0 copy.43
  (99 shorter events, 16.2 us)
Async XLA Ops:
  0.6 23.9 %copy-start = (f32[1,32]{1,0:T(1,128)S(1)}, f32[1,32]{1,0:T(1,128)}, u32[]{:S(2)}) copy-start(f32[1,32]{1,0:T(1,128)} %param.13) | copy-start | bytes 388
  0.6 10.7 %collective-permute-start = (bf16[1,128,2048]{2,1,0:T(8,128)(2,1)}, bf16[1,128,2048]{2,1,0:T(8,128)(2,1)S(1)}, u32[]{:S(2)}, u32[]{:S(2)}) collective-permute-start(bf16[1,128,2048]{2,1,0:T(8,128)(2,1)} %param.7), channel_id=1, source_target_pairs={{0,64},{64,128},{128,192},{192,256},{256,320},{320,384},{384,448},... | collective-permute-start | bytes 1572872 | tf_op jit(solution)/shard_map/ppermute | solution.py:23
  2.6 1.9 copy-start.10
  2.6 1.9 copy-start.11
  4.0 0.7 copy-start.15
  4.1 7.3 %copy-start.7 = (bf16[1,128,2048]{2,1,0:T(8,128)(2,1)S(1)}, bf16[1,128,2048]{2,1,0:T(8,128)(2,1)}, u32[]{:S(2)}) copy-start(bf16[1,128,2048]{2,1,0:T(8,128)(2,1)} %param.7) | copy-start | bytes 1572868
  11.8 0.7 copy-start.13
  17.3 39.6 %all-to-all-start = ((bf16[4,1296,128]{2,1,0:T(8,128)(2,1)}), bf16[4,1296,128]{2,1,0:T(8,128)(2,1)S(1)}, u32[]{:S(2)}, u32[]{:S(2)}) async-start(bf16[4,1296,128]{2,1,0:T(8,128)(2,1)} %concatenate.21), calls=%async_computation | async-start | bytes 2654208 | tf_op jit(solution)/shard_map/all_to_all | solution.py:129
  60.0 5.2 %copy-start.2 = (bf16[4,128,8,64]{1,3,2,0:T(8,128)(2,1)}, bf16[4,128,8,64]{1,3,2,0:T(8,128)(2,1)S(1)}, u32[]{:S(2)}) copy-start(bf16[4,128,8,64]{1,3,2,0:T(8,128)(2,1)S(1)} %copy.34) | copy-start | bytes 1572868
  64.9 1.0 copy-start.4
  64.9 67.1 %copy-start.12 = (f32[8]{0:T(128)}, f32[8]{0:T(128)S(1)}, u32[]{:S(2)}) copy-start(f32[8]{0:T(128)S(1)} %get-tuple-element.5) | copy-start | bytes 100
  67.7 28.5 %collective-permute-start.1 = (f32[8,128,64]{1,2,0:T(8,128)S(1)}, f32[8,128,64]{1,2,0:T(8,128)S(1)}, u32[]{:S(2)}, u32[]{:S(2)}) collective-permute-start(f32[8,128,64]{1,2,0:T(8,128)S(1)} %get-tuple-element.16), channel_id=1, source_target_pairs={{0,16},{16,32},{32,48},{48,0},{1,17},{17,33},{33,49},{49,1},{2,18}... | collective-permute-start | bytes 786440 | tf_op jit(solution)/shard_map/ppermute | solution.py:28
  79.3 31.5 %collective-permute-start.4 = (f32[8,128,64]{1,2,0:T(8,128)S(1)}, f32[8,128,64]{1,2,0:T(8,128)S(1)}, u32[]{:S(2)}, u32[]{:S(2)}) collective-permute-start(f32[8,128,64]{1,2,0:T(8,128)S(1)} %get-tuple-element.17), channel_id=1, source_target_pairs={{0,48},{16,0},{32,16},{48,32},{1,49},{17,1},{33,17},{49,33},{2,50}... | collective-permute-start | bytes 786440 | tf_op jit(solution)/shard_map/ppermute | solution.py:28
  96.3 35.7 %collective-permute-start.2 = (f32[8,128,64]{1,2,0:T(8,128)S(1)}, f32[8,128,64]{1,2,0:T(8,128)S(1)}, u32[]{:S(2)}, u32[]{:S(2)}) collective-permute-start(f32[8,128,64]{1,2,0:T(8,128)S(1)} %multiply_add_fusion.5), channel_id=1, source_target_pairs={{0,16},{16,32},{32,48},{48,0},{1,17},{17,33},{33,49},{49,1},{2,18}... | collective-permute-start | bytes 786440 | tf_op jit(solution)/shard_map/ppermute | solution.py:28
  132.1 28.2 %collective-permute-start.5 = (f32[8,128,64]{1,2,0:T(8,128)S(1)}, f32[8,128,64]{1,2,0:T(8,128)}, u32[]{:S(2)}, u32[]{:S(2)}) collective-permute-start(f32[8,128,64]{1,2,0:T(8,128)S(1)} %get-tuple-element.15), channel_id=1, source_target_pairs={{0,48},{16,0},{32,16},{48,32},{1,49},{17,1},{33,17},{49,33},{2,50}... | collective-permute-start | bytes 786440 | tf_op jit(solution)/shard_map/ppermute | solution.py:28
  151.7 15.8 %collective-permute-start.3 = (f32[8,128,64]{1,2,0:T(8,128)S(1)}, f32[8,128,64]{1,2,0:T(8,128)S(1)}, u32[]{:S(2)}, u32[]{:S(2)}) collective-permute-start(f32[8,128,64]{1,2,0:T(8,128)S(1)} %get-tuple-element.14), channel_id=1, source_target_pairs={{0,16},{16,32},{32,48},{48,0},{1,17},{17,33},{33,49},{49,1},{2,18}... | collective-permute-start | bytes 786440 | tf_op jit(solution)/shard_map/ppermute | solution.py:28
  157.8 9.8 %copy-start.1 = (f32[4,8,64,128]{3,2,1,0:T(8,128)S(1)}, f32[4,8,64,128]{3,2,1,0:T(8,128)}, u32[]{:S(2)}) copy-start(f32[4,8,64,128]{3,2,1,0:T(8,128)} %get-tuple-element.21) | copy-start | bytes 3145732
  162.1 16.3 %collective-permute-start.6 = (f32[8,128,64]{1,2,0:T(8,128)}, f32[8,128,64]{1,2,0:T(8,128)}, u32[]{:S(2)}, u32[]{:S(2)}) collective-permute-start(f32[8,128,64]{1,2,0:T(8,128)} %multiply_add_fusion.2), channel_id=1, source_target_pairs={{0,48},{16,0},{32,16},{48,32},{1,49},{17,1},{33,17},{49,33},{2,50}... | collective-permute-start | bytes 786440 | tf_op jit(solution)/shard_map/ppermute | solution.py:28
  171.2 1.0 copy-start.5
  171.2 1.1 copy-start.8
  171.2 1.1 copy-start.16
  177.2 2.3 %copy-start.14 = (pred[4,4]{0,1:T(4,128)(4,1)S(1)}, pred[4,4]{0,1:T(4,128)(4,1)}, u32[]{:S(2)}) copy-start(pred[4,4]{0,1:T(4,128)(4,1)} %fusion.61) | copy-start | bytes 52
  182.3 1.0 copy-start.3
  182.3 1.1 copy-start.9
  182.3 1.1 copy-start.17
  185.3 1.1 copy-start.6
